TPU v7x, 256 devices: a whole 4x4x8 slice. The times are simulated.
256 devices in a mesh: line: 16 (over x, y), plane: 16 (over z, core).
Axes of the slice: x: 4, y: 4, z: 8, core: 2. Of those that a mesh axis runs over, the one named last changes fastest.
Arguments:
- flux_x: float32 [1024, 5, 16384], P('line', None, 'plane'), may hold values from -1600 to 1600
- flux_z: float32 [1024, 5, 16384], P('line', None, 'plane'), may hold values from -1600 to 1600
- viscous: float32 [1024, 16384], P('line', 'plane'), may hold values from 4000 to 16000
- jacobian: float32 [1024, 5, 5, 16384], P('line', None, None, 'plane'), may hold values from -10 to 10
Outputs:
- delta: float32 [1024, 5, 16384], P('line', None, 'plane')
All inputs are finite; a program needn't handle non-finite values.
Results may differ from a plain program's by a relative error of at most 0.0003.
Values sent between devices are 32-bit elements; how exact they have to be, the bound alone decides.
No kernel may reach another device: no remote copies, remote signals or barrier semaphores. Data moves between devices by JAX's collectives and lax.ppermute only.
A program may use at most 192 MiB of HBM per device.

v0:
```python
import jax
import jax.numpy as jnp
from jax import lax
from jax.sharding import PartitionSpec as P

courant = 10.0


def padded(block, sides, width):
    for axis, dim in sides:
        count = lax.axis_size(axis)
        forward = [(i, i + 1) for i in range(count - 1)]
        backward = [(target, source) for source, target in forward]
        low = lax.ppermute(
            lax.slice_in_dim(block, block.shape[dim] - width, None, axis=dim), axis, forward
        )
        high = lax.ppermute(lax.slice_in_dim(block, 0, width, axis=dim), axis, backward)
        block = jnp.concatenate([low, block, high], axis=dim)
    return block


def from_behind(block, axis, distance):
    devices = range(lax.axis_size(axis))
    route = [(i - distance, i) for i in devices if i - distance in devices]
    return lax.ppermute(block, axis, route)


def combine_blocks(matrix, operand):
    return jnp.sum(matrix[:, :, None, :] * operand[None, :, :, :], axis=1)


def solve_small(matrix, columns):
    extent = matrix.shape[0]
    for column in range(extent):
        inverse = 1.0 / matrix[column, column]
        pivot_row = matrix[column] * inverse
        column_row = columns[column] * inverse
        factor = matrix[:, column]
        matrix = matrix - factor[:, None, :] * pivot_row[None]
        columns = columns - factor[:, None, :] * column_row[None]
        matrix = matrix.at[column].set(pivot_row)
        columns = columns.at[column].set(column_row)
    return columns


def cell_blocks(viscous, jacobian):
    identity = jnp.eye(5, dtype=jnp.float32)[:, :, None]
    spread = viscous[None, None, :]
    lower_block = -spread * identity - jacobian
    center_block = (1.0 + 2.0 * spread) * identity
    upper_block = -spread * identity + jacobian
    return (lower_block, center_block, upper_block)


def eliminate(previous, lower_block, center_block, upper_block, source):
    extent = center_block.shape[0]
    schur = center_block - combine_blocks(lower_block, previous[:, :extent])
    moved = source - combine_blocks(lower_block, previous[:, extent:])
    return solve_small(schur, jnp.concatenate([upper_block, moved], 1))


def back_substitute(factors, extent):

    def retreat(following, factor):
        current = factor[:, extent:] - combine_blocks(factor[:, :extent], following)
        return (current, current)

    initial = jnp.zeros(
        (factors.shape[1], factors.shape[2] - extent, factors.shape[3]), jnp.float32
    )
    _, values = lax.scan(retreat, initial, factors, reverse=True)
    return values


def local_factor(viscous, jacobian, source):
    cell_count = viscous.shape[0]
    line_count = viscous.shape[1]

    def advance(previous, inputs):
        vis_cell, jac_cell, src_cell, position = inputs
        lower_block, center_block, upper_block = cell_blocks(vis_cell, jac_cell)
        first_mask = (position == 0).astype(jnp.float32)
        last_mask = (position == cell_count - 1).astype(jnp.float32)
        columns = jnp.concatenate([src_cell, lower_block * first_mask, upper_block * last_mask], 1)
        result = eliminate(previous, lower_block, center_block, upper_block, columns)
        return (result, result)

    initial = jnp.zeros((5, 16, line_count), jnp.float32)
    _, factors = lax.scan(
        advance, initial, (viscous, jacobian, source, jnp.arange(cell_count, dtype=jnp.int32))
    )
    return factors


def reduced_blocks(head_rows, tail_rows):
    empty_block = jnp.zeros_like(head_rows[:, 1:6])
    coupling_prev = jnp.concatenate(
        [
            jnp.concatenate([empty_block, head_rows[:, 1:6]], 1),
            jnp.concatenate([empty_block, tail_rows[:, 1:6]], 1),
        ],
        0,
    )
    coupling_next = jnp.concatenate(
        [
            jnp.concatenate([head_rows[:, 6:11], empty_block], 1),
            jnp.concatenate([tail_rows[:, 6:11], empty_block], 1),
        ],
        0,
    )
    local_part = jnp.concatenate([head_rows[:, 0:1], tail_rows[:, 0:1]], 0)
    diagonal = jnp.eye(10, dtype=jnp.float32)[:, :, None] + jnp.zeros(
        (1, 1, head_rows.shape[2]), jnp.float32
    )
    return (coupling_prev, diagonal, coupling_next, local_part)


def per_device(flux_x, flux_z, viscous, jacobian):
    stream = padded(flux_x, (("line", 0),), 1)
    across = padded(flux_z, (("plane", 2),), 1)
    source = -0.5 * courant * (stream[2:] - stream[:-2]) - 0.5 * courant * (
        across[:, :, 2:] - across[:, :, :-2]
    )
    factors = local_factor(viscous, jacobian, source[:, :, None, :])
    solved = back_substitute(factors, 5)
    head_rows = solved[0]
    tail_rows = solved[-1]
    line_count = viscous.shape[1]
    partitions = lax.axis_size("line")
    coupling_prev, diagonal, coupling_next, local_part = reduced_blocks(head_rows, tail_rows)

    def forward_turn(iteration, mine):
        arrived = from_behind(mine, "line", 1)
        return eliminate(arrived, coupling_prev, diagonal, coupling_next, local_part)

    state = lax.fori_loop(0, partitions, forward_turn, jnp.zeros((10, 11, line_count), jnp.float32))

    def backward_turn(iteration, mine):
        arrived = from_behind(mine, "line", -1)
        return state[:, 10:] - combine_blocks(state[:, :10], arrived)

    ends = lax.fori_loop(0, partitions, backward_turn, jnp.zeros((10, 1, line_count), jnp.float32))
    before = from_behind(ends[5:], "line", 1)
    after = from_behind(ends[:5], "line", -1)
    delta = (
        solved[:, :, 0]
        - jnp.sum(solved[:, :, 1:6] * before[:, 0][None, None], axis=2)
        - jnp.sum(solved[:, :, 6:11] * after[:, 0][None, None], axis=2)
    )
    return delta


def solution(mesh):
    placed = (
        P("line", None, "plane"),
        P("line", None, "plane"),
        P("line", "plane"),
        P("line", None, None, "plane"),
    )
    return jax.shard_map(
        per_device, mesh=mesh, in_specs=placed, out_specs=P("line", None, "plane"), check_vma=False
    )
```

profile of v0, /device:TPU:96, one launch (start us, length us, event | category | flops | bytes accessed | tf_op | source)
XLA Modules:
  0.0 1092.8 jit_solution(17676864555278931995)
XLA Ops:
  17.3 417.5 %while.85 = (s32[]{:T(128)}, f32[5,16,1024]{2,1,0:T(8,128)S(1)}, f32[64,5,16,1024]{3,2,1,0:T(8,128)}, f32[64,1024]{1,0:T(8,128)}, f32[64,5,5,1024]{3,0,2,1:T(8,1...) while((s32[]{:T(128)}, f32[5,16,1024]{2,1,0:T(8,128)S(1)}, ...), condition=%wide.region_3.4_spmd, body=%wide.region_0.3_spmd.sunk | while | flops 2488376 | bytes 11473969 | solution.py:89
  434.8 9.8 broadcast_in_dim.31
  444.6 129.4 %while.87 = (s32[]{:T(128)}, f32[5,11,1024]{2,1,0:T(8,128)S(1)}, f32[64,5,11,1024]{3,2,1,0:T(8,128)}, f32[64,5,16,1024]{3,2,1,0:T(8,128)}, s32[]{:T(128)}, /*index=5*/s32[]{:T(128)}, s32[]{:T(128)}) while((s32[]{:T(128)}, f32[5,11,1024]{2,1,0:T(8,128)S(1)}, f32[64,5,11,1024]{3,2,1,0:T(8,128)}, f32[64,5,16,1024]{3,2,1,0:T(8,128)}, ...), condition=%wide.region_6.7_spmd.clone, body=%wide.region_4.6_spmd.clone.sunk | while | flops 619524 | bytes 2867307 | solution.py:71
  575.5 330.0 %while.86 = (s32[]{:T(128)}, f32[10,11,1024]{2,1,0:T(8,128)S(1)}, f32[10,10,1024]{2,1,0:T(8,128)S(1)}, f32[10,1,1024]{2,1,0:T(1,128)S(1)}, f32[10,10,1024]{2,1,0:T(8,128)S(1)}, /*index=5*/f32[10,10]{1,0:T(8,128)S(1)}, s32[]{:T(128)}) while((s32[]{:T(128)}, f32[10,11,1024]{2,1,0:T(8,128)S(1)}, f32[10,10,1024]{2,1,0:T(8,128)S(1)}, ...), condition=%wide.region_10.11_spmd.clone, body=%wide.region_7.10_spmd.clone.sunk | while | flops 6903810 | bytes 29651460 | solution.py:136
  579.7 14.8 %collective-permute-done = f32[10,11,1024]{2,1,0:T(8,128)S(1)} collective-permute-done((f32[10,11,1024]{2,1,0:T(8,128)S(1)}, f32[10,11,1024]{2,1,0:T(8,128)S(1)}, u32[]{:S(2)}, u32[]{:S(2)}) %collective-permute-start) | collective-permute-done | bytes 450592 | tf_op jit(solution)/shard_map/while/body/eval_jaxpr/ppermute | solution.py:25
  603.2 14.2 %collective-permute-done = f32[10,11,1024]{2,1,0:T(8,128)S(1)} collective-permute-done((f32[10,11,1024]{2,1,0:T(8,128)S(1)}, f32[10,11,1024]{2,1,0:T(8,128)S(1)}, u32[]{:S(2)}, u32[]{:S(2)}) %collective-permute-start) | collective-permute-done | bytes 450592 | tf_op jit(solution)/shard_map/while/body/eval_jaxpr/ppermute | solution.py:25
  626.1 13.4 %collective-permute-done = f32[10,11,1024]{2,1,0:T(8,128)S(1)} collective-permute-done((f32[10,11,1024]{2,1,0:T(8,128)S(1)}, f32[10,11,1024]{2,1,0:T(8,128)S(1)}, u32[]{:S(2)}, u32[]{:S(2)}) %collective-permute-start) | collective-permute-done | bytes 450592 | tf_op jit(solution)/shard_map/while/body/eval_jaxpr/ppermute | solution.py:25
  649.8 12.7 %collective-permute-done = f32[10,11,1024]{2,1,0:T(8,128)S(1)} collective-permute-done((f32[10,11,1024]{2,1,0:T(8,128)S(1)}, f32[10,11,1024]{2,1,0:T(8,128)S(1)}, u32[]{:S(2)}, u32[]{:S(2)}) %collective-permute-start) | collective-permute-done | bytes 450592 | tf_op jit(solution)/shard_map/while/body/eval_jaxpr/ppermute | solution.py:25
  672.5 11.5 %collective-permute-done = f32[10,11,1024]{2,1,0:T(8,128)S(1)} collective-permute-done((f32[10,11,1024]{2,1,0:T(8,128)S(1)}, f32[10,11,1024]{2,1,0:T(8,128)S(1)}, u32[]{:S(2)}, u32[]{:S(2)}) %collective-permute-start) | collective-permute-done | bytes 450592 | tf_op jit(solution)/shard_map/while/body/eval_jaxpr/ppermute | solution.py:25
  688.2 6.5 collective-permute-start
  694.8 10.6 collective-permute-done
  709.6 6.5 collective-permute-start
  716.1 9.7 collective-permute-done
  730.0 6.5 collective-permute-start
  736.6 8.8 collective-permute-done
  749.6 6.5 collective-permute-start
  756.1 8.0 collective-permute-done
  774.9 8.0 collective-permute-done
  793.7 8.0 collective-permute-done
  805.9 6.5 collective-permute-start
  812.5 8.0 collective-permute-done
  824.7 6.5 collective-permute-start
  831.3 8.3 collective-permute-done
  843.8 6.8 collective-permute-start
  850.6 9.4 collective-permute-done
  864.2 7.0 collective-permute-start
  871.2 10.4 collective-permute-done
  885.8 7.4 collective-permute-start
  893.3 8.0 collective-permute-done
  905.5 135.7 %while.88 = (s32[]{:T(128)}, f32[10,1,1024]{2,1,0:T(1,128)S(1)}, f32[10,11,1024]{2,1,0:T(8,128)S(1)}, s32[]{:T(128)}, s32[]{:T(128)}) while((s32[]{:T(128)}, f32[10,1,1024]{2,1,0:T(1,128)S(1)}, f32[10,11,1024]{2,1,0:T(8,128)S(1)}, s32[]{:T(128)}, s32[]{:T(128)}) %tuple.254), condition=%wide.region_13.14_spmd.clone, body=%wide.region_11.13_spmd.clone.sunk | while | flops 215043 | bytes 942191 | solution.py:142
  906.9 7.8 collective-permute-done.1
  916.2 7.8 collective-permute-done.1
  925.6 6.8 collective-permute-done.1
  934.0 7.2 collective-permute-done.1
  942.8 6.7 collective-permute-done.1
  951.1 6.7 collective-permute-done.1
  959.4 6.8 collective-permute-done.1
  967.7 7.0 collective-permute-done.1
  976.3 6.5 collective-permute-done.1
  984.4 6.7 collective-permute-done.1
  992.7 6.7 collective-permute-done.1
  1001.0 6.7 collective-permute-done.1
  1009.3 6.9 collective-permute-done.1
  1025.9 6.8 collective-permute-done.1
  1034.3 6.7 collective-permute-done.1
  1042.5 6.8 collective-permute-start.6
  1049.4 20.8 %copy.24 = f32[64,5,11,1024]{3,1,0,2:T(8,128)} copy(f32[64,5,11,1024]{3,2,1,0:T(8,128)} %get-tuple-element.701) | data formatting | bytes 28835840 | tf_op jit(solution)/shard_map/while | solution.py:71
  1070.2 18.5 %multiply_reduce_fusion.7 = (f32[64,5,1024]{2,1,0:T(8,128)S(1)}, f32[64,5,1024]{2,1,0:T(8,128)S(1)}) fusion(f32[64,5,11,1024]{3,2,1,0:T(8,128)} %get-tuple-element.701, f32[5,1024]{1,0:T(8,128)S(1)} %bitcast.396, f32[5,1024]{1,0:T(8,128)S(1)} %bitcast.395), kind=kLoop, calls=%fused_computation.183 | loop fusion | flops 5898240 | bytes 15769600 | tf_op jit(solution)/shard_map/reduce_sum | solution.py:147
  (5433 shorter events, 583.7 us)
Async XLA Ops:
  1.1 11.3 %collective-permute-start.4 = (f32[64,5,1]{2,0,1:T(8,128)S(1)}, f32[64,5,1]{2,0,1:T(8,128)S(1)}, u32[]{:S(2)}, u32[]{:S(2)}) collective-permute-start(f32[64,5,1]{2,0,1:T(8,128)S(1)} %get-tuple-element.830), channel_id=1, source_target_pairs={{1,0},{2,1},{3,2},{4,3},{5,4},{6,5},{7,6},{8,7},{9,8},{10,9},{11,1... | collective-permute-start | bytes 3848 | tf_op jit(solution)/shard_map/ppermute | solution.py:17
  3.0 9.4 collective-permute-start.5
  6.5 5.9 collective-permute-start.2
  7.8 6.0 collective-permute-start.3
  575.5 19.1 %collective-permute-start = (f32[10,11,1024]{2,1,0:T(8,128)S(1)}, f32[10,11,1024]{2,1,0:T(8,128)S(1)}, u32[]{:S(2)}, u32[]{:S(2)}) collective-permute-start(f32[10,11,1024]{2,1,0:T(8,128)S(1)} %get-tuple-element.1043), channel_id=1, source_target_pairs={{0,16},{16,32},{32,48},{48,64},{64,80},{80,96},{96,112},{112,128},... | collective-permute-start | bytes 1351688 | tf_op jit(solution)/shard_map/while/body/eval_jaxpr/ppermute | solution.py:25
  598.8 18.6 %collective-permute-start = (f32[10,11,1024]{2,1,0:T(8,128)S(1)}, f32[10,11,1024]{2,1,0:T(8,128)S(1)}, u32[]{:S(2)}, u32[]{:S(2)}) collective-permute-start(f32[10,11,1024]{2,1,0:T(8,128)S(1)} %get-tuple-element.1043), channel_id=1, source_target_pairs={{0,16},{16,32},{32,48},{48,64},{64,80},{80,96},{96,112},{112,128},... | collective-permute-start | bytes 1351688 | tf_op jit(solution)/shard_map/while/body/eval_jaxpr/ppermute | solution.py:25
  621.6 17.9 %collective-permute-start = (f32[10,11,1024]{2,1,0:T(8,128)S(1)}, f32[10,11,1024]{2,1,0:T(8,128)S(1)}, u32[]{:S(2)}, u32[]{:S(2)}) collective-permute-start(f32[10,11,1024]{2,1,0:T(8,128)S(1)} %get-tuple-element.1043), channel_id=1, source_target_pairs={{0,16},{16,32},{32,48},{48,64},{64,80},{80,96},{96,112},{112,128},... | collective-permute-start | bytes 1351688 | tf_op jit(solution)/shard_map/while/body/eval_jaxpr/ppermute | solution.py:25
  643.7 18.9 %collective-permute-start = (f32[10,11,1024]{2,1,0:T(8,128)S(1)}, f32[10,11,1024]{2,1,0:T(8,128)S(1)}, u32[]{:S(2)}, u32[]{:S(2)}) collective-permute-start(f32[10,11,1024]{2,1,0:T(8,128)S(1)} %get-tuple-element.1043), channel_id=1, source_target_pairs={{0,16},{16,32},{32,48},{48,64},{64,80},{80,96},{96,112},{112,128},... | collective-permute-start | bytes 1351688 | tf_op jit(solution)/shard_map/while/body/eval_jaxpr/ppermute | solution.py:25
  666.8 17.3 %collective-permute-start = (f32[10,11,1024]{2,1,0:T(8,128)S(1)}, f32[10,11,1024]{2,1,0:T(8,128)S(1)}, u32[]{:S(2)}, u32[]{:S(2)}) collective-permute-start(f32[10,11,1024]{2,1,0:T(8,128)S(1)} %get-tuple-element.1043), channel_id=1, source_target_pairs={{0,16},{16,32},{32,48},{48,64},{64,80},{80,96},{96,112},{112,128},... | collective-permute-start | bytes 1351688 | tf_op jit(solution)/shard_map/while/body/eval_jaxpr/ppermute | solution.py:25
  688.2 17.2 %collective-permute-start = (f32[10,11,1024]{2,1,0:T(8,128)S(1)}, f32[10,11,1024]{2,1,0:T(8,128)S(1)}, u32[]{:S(2)}, u32[]{:S(2)}) collective-permute-start(f32[10,11,1024]{2,1,0:T(8,128)S(1)} %get-tuple-element.1043), channel_id=1, source_target_pairs={{0,16},{16,32},{32,48},{48,64},{64,80},{80,96},{96,112},{112,128},... | collective-permute-start | bytes 1351688 | tf_op jit(solution)/shard_map/while/body/eval_jaxpr/ppermute | solution.py:25
  709.6 16.2 %collective-permute-start = (f32[10,11,1024]{2,1,0:T(8,128)S(1)}, f32[10,11,1024]{2,1,0:T(8,128)S(1)}, u32[]{:S(2)}, u32[]{:S(2)}) collective-permute-start(f32[10,11,1024]{2,1,0:T(8,128)S(1)} %get-tuple-element.1043), channel_id=1, source_target_pairs={{0,16},{16,32},{32,48},{48,64},{64,80},{80,96},{96,112},{112,128},... | collective-permute-start | bytes 1351688 | tf_op jit(solution)/shard_map/while/body/eval_jaxpr/ppermute | solution.py:25
  730.0 15.3 %collective-permute-start = (f32[10,11,1024]{2,1,0:T(8,128)S(1)}, f32[10,11,1024]{2,1,0:T(8,128)S(1)}, u32[]{:S(2)}, u32[]{:S(2)}) collective-permute-start(f32[10,11,1024]{2,1,0:T(8,128)S(1)} %get-tuple-element.1043), channel_id=1, source_target_pairs={{0,16},{16,32},{32,48},{48,64},{64,80},{80,96},{96,112},{112,128},... | collective-permute-start | bytes 1351688 | tf_op jit(solution)/shard_map/while/body/eval_jaxpr/ppermute | solution.py:25
  749.6 14.6 %collective-permute-start = (f32[10,11,1024]{2,1,0:T(8,128)S(1)}, f32[10,11,1024]{2,1,0:T(8,128)S(1)}, u32[]{:S(2)}, u32[]{:S(2)}) collective-permute-start(f32[10,11,1024]{2,1,0:T(8,128)S(1)} %get-tuple-element.1043), channel_id=1, source_target_pairs={{0,16},{16,32},{32,48},{48,64},{64,80},{80,96},{96,112},{112,128},... | collective-permute-start | bytes 1351688 | tf_op jit(solution)/shard_map/while/body/eval_jaxpr/ppermute | solution.py:25
  768.4 14.6 %collective-permute-start = (f32[10,11,1024]{2,1,0:T(8,128)S(1)}, f32[10,11,1024]{2,1,0:T(8,128)S(1)}, u32[]{:S(2)}, u32[]{:S(2)}) collective-permute-start(f32[10,11,1024]{2,1,0:T(8,128)S(1)} %get-tuple-element.1043), channel_id=1, source_target_pairs={{0,16},{16,32},{32,48},{48,64},{64,80},{80,96},{96,112},{112,128},... | collective-permute-start | bytes 1351688 | tf_op jit(solution)/shard_map/while/body/eval_jaxpr/ppermute | solution.py:25
  787.1 14.6 %collective-permute-start = (f32[10,11,1024]{2,1,0:T(8,128)S(1)}, f32[10,11,1024]{2,1,0:T(8,128)S(1)}, u32[]{:S(2)}, u32[]{:S(2)}) collective-permute-start(f32[10,11,1024]{2,1,0:T(8,128)S(1)} %get-tuple-element.1043), channel_id=1, source_target_pairs={{0,16},{16,32},{32,48},{48,64},{64,80},{80,96},{96,112},{112,128},... | collective-permute-start | bytes 1351688 | tf_op jit(solution)/shard_map/while/body/eval_jaxpr/ppermute | solution.py:25
  805.9 14.6 %collective-permute-start = (f32[10,11,1024]{2,1,0:T(8,128)S(1)}, f32[10,11,1024]{2,1,0:T(8,128)S(1)}, u32[]{:S(2)}, u32[]{:S(2)}) collective-permute-start(f32[10,11,1024]{2,1,0:T(8,128)S(1)} %get-tuple-element.1043), channel_id=1, source_target_pairs={{0,16},{16,32},{32,48},{48,64},{64,80},{80,96},{96,112},{112,128},... | collective-permute-start | bytes 1351688 | tf_op jit(solution)/shard_map/while/body/eval_jaxpr/ppermute | solution.py:25
  824.7 14.8 %collective-permute-start = (f32[10,11,1024]{2,1,0:T(8,128)S(1)}, f32[10,11,1024]{2,1,0:T(8,128)S(1)}, u32[]{:S(2)}, u32[]{:S(2)}) collective-permute-start(f32[10,11,1024]{2,1,0:T(8,128)S(1)} %get-tuple-element.1043), channel_id=1, source_target_pairs={{0,16},{16,32},{32,48},{48,64},{64,80},{80,96},{96,112},{112,128},... | collective-permute-start | bytes 1351688 | tf_op jit(solution)/shard_map/while/body/eval_jaxpr/ppermute | solution.py:25
  843.8 16.2 %collective-permute-start = (f32[10,11,1024]{2,1,0:T(8,128)S(1)}, f32[10,11,1024]{2,1,0:T(8,128)S(1)}, u32[]{:S(2)}, u32[]{:S(2)}) collective-permute-start(f32[10,11,1024]{2,1,0:T(8,128)S(1)} %get-tuple-element.1043), channel_id=1, source_target_pairs={{0,16},{16,32},{32,48},{48,64},{64,80},{80,96},{96,112},{112,128},... | collective-permute-start | bytes 1351688 | tf_op jit(solution)/shard_map/while/body/eval_jaxpr/ppermute | solution.py:25
  864.2 17.4 %collective-permute-start = (f32[10,11,1024]{2,1,0:T(8,128)S(1)}, f32[10,11,1024]{2,1,0:T(8,128)S(1)}, u32[]{:S(2)}, u32[]{:S(2)}) collective-permute-start(f32[10,11,1024]{2,1,0:T(8,128)S(1)} %get-tuple-element.1043), channel_id=1, source_target_pairs={{0,16},{16,32},{32,48},{48,64},{64,80},{80,96},{96,112},{112,128},... | collective-permute-start | bytes 1351688 | tf_op jit(solution)/shard_map/while/body/eval_jaxpr/ppermute | solution.py:25
  885.8 15.5 %collective-permute-start = (f32[10,11,1024]{2,1,0:T(8,128)S(1)}, f32[10,11,1024]{2,1,0:T(8,128)S(1)}, u32[]{:S(2)}, u32[]{:S(2)}) collective-permute-start(f32[10,11,1024]{2,1,0:T(8,128)S(1)} %get-tuple-element.1043), channel_id=1, source_target_pairs={{0,16},{16,32},{32,48},{48,64},{64,80},{80,96},{96,112},{112,128},... | collective-permute-start | bytes 1351688 | tf_op jit(solution)/shard_map/while/body/eval_jaxpr/ppermute | solution.py:25
  905.6 9.1 collective-permute-start.1
  914.9 9.1 collective-permute-start.1
  924.3 8.2 collective-permute-start.1
  932.7 8.5 collective-permute-start.1
  941.5 8.0 collective-permute-start.1
  949.8 8.0 collective-permute-start.1
  958.1 8.1 collective-permute-start.1
  966.4 8.3 collective-permute-start.1
  975.0 7.8 collective-permute-start.1
  983.1 8.0 collective-permute-start.1
  991.4 8.0 collective-permute-start.1
  999.7 8.0 collective-permute-start.1
  1008.0 8.2 collective-permute-start.1
  1016.5 7.8 collective-permute-start.1
  1024.6 8.1 collective-permute-start.1
  1033.0 8.0 collective-permute-start.1
  1041.2 29.0 %collective-permute-start.7 = (f32[5,1,1024]{2,1,0:T(1,128)S(1)}, f32[5,1,1024]{2,1,0:T(1,128)S(1)}, u32[]{:S(2)}, u32[]{:S(2)}) collective-permute-start(f32[5,1,1024]{2,1,0:T(1,128)S(1)} %get-tuple-element.836), channel_id=1, source_target_pairs={{16,0},{32,16},{48,32},{64,48},{80,64},{96,80},{112,96},{128,112},... | collective-permute-start | bytes 61448 | tf_op jit(solution)/shard_map/ppermute | solution.py:25
  1042.5 27.7 %collective-permute-start.6 = (f32[5,1,1024]{2,1,0:T(1,128)S(1)}, f32[5,1,1024]{2,1,0:T(1,128)S(1)}, u32[]{:S(2)}, u32[]{:S(2)}) collective-permute-start(f32[5,1,1024]{2,1,0:T(1,128)S(1)} %get-tuple-element.837), channel_id=1, source_target_pairs={{0,16},{16,32},{32,48},{48,64},{64,80},{80,96},{96,112},{112,128},... | collective-permute-start | bytes 61448 | tf_op jit(solution)/shard_map/ppermute | solution.py:25
where the time goes:
time: 1110 us; the launch traced here: 1090 us
  local copies, waits for them, and re-layouts  292 us (26%)
  waiting for transfers between devices  276 us (25%)
  other arithmetic  263 us (24%)
  starting transfers between devices  137 us (12%)
  loops' own time  124 us (11%)
    ppermute x34, waiting for transfers between devices, from_behind(): return lax.ppermute(block, axis, route)  274 us
    ppermute x34, starting transfers between devices, from_behind(): return lax.ppermute(block, axis, route)  127 us
    dynamic_slice x128, local copies, waits for them, and re-layouts, local_factor(): lax.scan(advance, initial, (viscous, jacobian, source, jnp.arange(cell_co...  120 us
    another operation x1, loops' own time, local_factor(): lax.scan(advance, initial, (viscous, jacobian, source, jnp.arange(cell_co...  111 us
    squeeze x64, local copies, waits for them, and re-layouts, back_substitute(): _, values = lax.scan(retreat, initial, factors, reverse=True)  63.6 us
    dynamic_update_slice x64, other arithmetic, back_substitute(): _, values = lax.scan(retreat, initial, factors, reverse=True)  52.1 us
    add x64, other arithmetic, cell_blocks(): center_block = (1.0 + 2.0 * spread) * identity  49.6 us
    dynamic_update_slice x64, local copies, waits for them, and re-layouts, local_factor(): lax.scan(advance, initial, (viscous, jacobian, source, jnp.arange(cell_co...  48.6 us

commit v1 on v0

v1 whole, which is shorter than its diff:
```python
import jax
import jax.numpy as jnp
from jax import lax
from jax.experimental import pallas as pl
from jax.experimental.pallas import tpu as pltpu
from jax.sharding import PartitionSpec as P

courant = 10.0
NV = 5


def padded(block, sides, width):
    for axis, dim in sides:
        count = lax.axis_size(axis)
        forward = [(i, i + 1) for i in range(count - 1)]
        backward = [(target, source) for source, target in forward]
        low = lax.ppermute(
            lax.slice_in_dim(block, block.shape[dim] - width, None, axis=dim), axis, forward
        )
        high = lax.ppermute(lax.slice_in_dim(block, 0, width, axis=dim), axis, backward)
        block = jnp.concatenate([low, block, high], axis=dim)
    return block


def matmul(a, b, rows, inner, cols):
    out = []
    for r in range(rows):
        line = []
        for c in range(cols):
            acc = a[r][0] * b[0][c]
            for k in range(1, inner):
                acc = acc + a[r][k] * b[k][c]
            line.append(acc)
        out.append(line)
    return out


def gauss_jordan(matrix, columns):
    matrix = [row[:] for row in matrix]
    columns = [row[:] for row in columns]
    for k in range(NV):
        inverse = 1.0 / matrix[k][k]
        pivot = [matrix[k][j] * inverse for j in range(k + 1, NV)]
        chosen = [x * inverse for x in columns[k]]
        for r in range(NV):
            if r == k:
                continue
            factor = matrix[r][k]
            for jj, j in enumerate(range(k + 1, NV)):
                matrix[r][j] = matrix[r][j] - factor * pivot[jj]
            columns[r] = [x - factor * y for x, y in zip(columns[r], chosen)]
        matrix[k] = [None] * (k + 1) + pivot
        columns[k] = chosen
    return columns


def grid_of(flat, rows, cols):
    return [[flat[r * cols + c] for c in range(cols)] for r in range(rows)]


def flat_of(grid):
    return [x for row in grid for x in row]


def factor_kernel(vis_ref, jac_ref, src_ref, out_ref):
    cells = vis_ref.shape[0]
    tile = vis_ref.shape[1:]
    zero = jnp.zeros(tile, jnp.float32)
    one = jnp.ones(tile, jnp.float32)

    def forward(i, carry):
        c_prev = grid_of(carry[0:25], NV, NV)
        g_prev = [[x] for x in carry[25:30]]
        w_prev = grid_of(carry[30:55], NV, NV)
        spread = vis_ref[i]
        jac = [[jac_ref[i, a * NV + b] for b in range(NV)] for a in range(NV)]
        lower = [[(-spread - jac[a][b]) if a == b else (-jac[a][b]) for b in range(NV)] for a in range(NV)]
        upper = [[(-spread + jac[a][b]) if a == b else jac[a][b] for b in range(NV)] for a in range(NV)]
        centre = 1.0 + 2.0 * spread
        lc = matmul(lower, c_prev, NV, NV, NV)
        schur = [[(centre - lc[a][c]) if a == c else (-lc[a][c]) for c in range(NV)] for a in range(NV)]
        lg = matmul(lower, g_prev, NV, NV, 1)
        lw = matmul(lower, w_prev, NV, NV, NV)
        cols = []
        for a in range(NV):
            cols.append(upper[a] + [src_ref[i, a] - lg[a][0]] + [-x for x in lw[a]])
        sol = gauss_jordan(schur, cols)
        c_new = [row[0:NV] for row in sol]
        g_new = [row[NV] for row in sol]
        w_new = [row[NV + 1:] for row in sol]
        flat = flat_of(c_new) + g_new + flat_of(w_new)
        for k in range(55):
            out_ref[i, k] = flat[k]
        return tuple(flat)

    init = [zero] * 30 + flat_of([[(-one if a == b else zero) for b in range(NV)] for a in range(NV)])
    lax.fori_loop(0, cells, forward, tuple(init))

    def backward(step, carry):
        i = cells - 1 - step
        nxt = [[carry[a]] + list(carry[5 + a * 5:10 + a * 5]) + list(carry[30 + a * 5:35 + a * 5]) for a in range(NV)]
        c_i = [[out_ref[i, a * NV + b] for b in range(NV)] for a in range(NV)]
        g_i = [out_ref[i, 25 + a] for a in range(NV)]
        w_i = [[out_ref[i, 30 + a * NV + b] for b in range(NV)] for a in range(NV)]
        prod = matmul(c_i, nxt, NV, NV, 11)
        y = [g_i[a] - prod[a][0] for a in range(NV)]
        w = [[w_i[a][b] - prod[a][1 + b] for b in range(NV)] for a in range(NV)]
        v = [[-prod[a][6 + b] for b in range(NV)] for a in range(NV)]
        flat = y + flat_of(w) + flat_of(v)
        for k in range(55):
            out_ref[i, k] = flat[k]
        return tuple(flat)

    init = [zero] * 30 + flat_of([[(-one if a == b else zero) for b in range(NV)] for a in range(NV)])
    lax.fori_loop(0, cells, backward, tuple(init))


def reduced_kernel(tail_ref, head_ref, out_ref, keep_ref):
    steps = tail_ref.shape[0]
    lanes = tail_ref.shape[2]

    def row(ref, q, k):
        return ref[q, k:k + 1, :]

    def forward(q, carry):
        x_prev = grid_of(carry[0:25], NV, NV)
        u_prev = [[x] for x in carry[25:30]]
        y63 = [row(tail_ref, q, a) for a in range(NV)]
        w63 = [[row(tail_ref, q, 5 + a * NV + b) for b in range(NV)] for a in range(NV)]
        v63 = [[row(tail_ref, q, 30 + a * NV + b) for b in range(NV)] for a in range(NV)]
        y0 = [row(head_ref, q, a) for a in range(NV)]
        w0 = [[row(head_ref, q, 5 + a * NV + b) for b in range(NV)] for a in range(NV)]
        v0 = [[row(head_ref, q, 30 + a * NV + b) for b in range(NV)] for a in range(NV)]
        wx = matmul(w63, x_prev, NV, NV, NV)
        m = [[v63[a][b] - wx[a][b] for b in range(NV)] for a in range(NV)]
        wu = matmul(w63, u_prev, NV, NV, 1)
        av = [[y63[a] - wu[a][0]] for a in range(NV)]
        wm = matmul(w0, m, NV, NV, NV)
        k_mat = [[(1.0 - wm[a][b]) if a == b else (-wm[a][b]) for b in range(NV)] for a in range(NV)]
        wa = matmul(w0, av, NV, NV, 1)
        cols = [v0[a] + [y0[a] - wa[a][0]] for a in range(NV)]
        sol = gauss_jordan(k_mat, cols)
        y_new = [r[0:NV] for r in sol]
        v_new = [[r[NV]] for r in sol]
        my = matmul(m, y_new, NV, NV, NV)
        x_new = [[-my[a][b] for b in range(NV)] for a in range(NV)]
        mv = matmul(m, v_new, NV, NV, 1)
        u_new = [av[a][0] - mv[a][0] for a in range(NV)]
        flat = flat_of(x_new) + flat_of(y_new) + u_new + [r[0] for r in v_new]
        for k in range(60):
            keep_ref[q, k:k + 1, :] = flat[k]
        return tuple(flat[0:25] + u_new)

    zero = jnp.zeros((1, lanes), jnp.float32)
    lax.fori_loop(0, steps, forward, tuple([zero] * 30))

    h_next = [[zero] for _ in range(NV)]
    for q in range(steps - 1, -1, -1):
        x_q = [[keep_ref[q, a * NV + b:a * NV + b + 1, :] for b in range(NV)] for a in range(NV)]
        y_q = [[keep_ref[q, 25 + a * NV + b:26 + a * NV + b, :] for b in range(NV)] for a in range(NV)]
        u_q = [keep_ref[q, 50 + a:51 + a, :] for a in range(NV)]
        v_q = [keep_ref[q, 55 + a:56 + a, :] for a in range(NV)]
        xh = matmul(x_q, h_next, NV, NV, 1)
        yh = matmul(y_q, h_next, NV, NV, 1)
        t_prev = [u_q[a] - xh[a][0] for a in range(NV)]
        h_here = [v_q[a] - yh[a][0] for a in range(NV)]
        if q <= steps - 2:
            for a in range(NV):
                out_ref[q, a:a + 1, :] = t_prev[a]
        if q >= 1:
            for a in range(NV):
                out_ref[q - 1, 5 + a:6 + a, :] = h_here[a]
        h_next = [[x] for x in h_here]


def whole(shape):
    return jax.ShapeDtypeStruct(shape, jnp.float32)


def per_device(flux_x, flux_z, viscous, jacobian):
    cells, line_count = viscous.shape
    rows = line_count // 128
    parts = lax.axis_size("line")
    stream = padded(flux_x, (("line", 0),), 1)
    across = padded(flux_z, (("plane", 2),), 1)
    source = -0.5 * courant * (stream[2:] - stream[:-2]) - 0.5 * courant * (
        across[:, :, 2:] - across[:, :, :-2]
    )
    src4 = source.reshape(cells, NV, rows, 128)
    jac4 = jacobian.reshape(cells, NV * NV, rows, 128)
    vis3 = viscous.reshape(cells, rows, 128)
    vmem = pl.BlockSpec(memory_space=pltpu.VMEM)
    factors = pl.pallas_call(
        factor_kernel,
        out_shape=whole((cells, 55, rows, 128)),
        in_specs=[vmem, vmem, vmem],
        out_specs=vmem,
        compiler_params=pltpu.CompilerParams(vmem_limit_bytes=60 * 1024 * 1024),
    )(vis3, jac4, src4)

    ends = jnp.stack([factors[0], factors[cells - 1]]).reshape(2 * 55, line_count)
    chunk = line_count // parts
    gathered = lax.all_to_all(ends, "line", 1, 0, tiled=True).reshape(parts, 2, 55, chunk)
    empty = jnp.zeros((1, 55, chunk), jnp.float32)
    tails = jnp.concatenate([empty, gathered[:, 1]], 0)
    heads = jnp.concatenate([gathered[:, 0], empty], 0)
    answers = pl.pallas_call(
        reduced_kernel,
        out_shape=whole((parts, 10, chunk)),
        in_specs=[vmem, vmem],
        out_specs=vmem,
        scratch_shapes=[pltpu.VMEM((parts + 1, 60, chunk), jnp.float32)],
    )(tails, heads)
    back = lax.all_to_all(answers, "line", 0, 0, tiled=True)
    bounds = jnp.moveaxis(back, 0, 1).reshape(10, rows, 128)
    before = bounds[0:NV]
    after = bounds[NV:]
    local = factors[:, 0:NV]
    w = factors[:, 5:30].reshape(cells, NV, NV, rows, 128)
    v = factors[:, 30:55].reshape(cells, NV, NV, rows, 128)
    delta = local - jnp.sum(w * before[None, None], axis=2) - jnp.sum(v * after[None, None], axis=2)
    return delta.reshape(cells, NV, line_count)


def solution(mesh):
    placed = (
        P("line", None, "plane"),
        P("line", None, "plane"),
        P("line", "plane"),
        P("line", None, None, "plane"),
    )
    return jax.shard_map(
        per_device, mesh=mesh, in_specs=placed, out_specs=P("line", None, "plane"), check_vma=False
    )
```

time: 1110 us -> 111 us (0.10)
  the two profiles are of different devices: /device:TPU:96 before, /device:TPU:1 now
where the time goes in v1:
time: 111 us; the launch traced here: 110 us
  local copies, waits for them, and re-layouts  32.7 us (29%)
  Pallas kernels  31.4 us (28%)
  blocking collectives  19.7 us (18%)
  starting transfers between devices  16.4 us (15%)
  other arithmetic  10 us (9%)
    pallas_call x1, Pallas kernels, per_device(): pl.pallas_call(factor_kernel, out_shape=whole((cells, 55, rows, 128)), in...  26 us
    all_to_all x1, blocking collectives, per_device(): lax.all_to_all(ends, 'line', 1, 0, tiled=True).reshape(parts, 2, 55, chunk)  19.7 us
    slice x1, local copies, waits for them, and re-layouts, per_device(): w = factors[:, 5:30].reshape(cells, NV, NV, rows, 128)  10.4 us
    unnamed x11, local copies, waits for them, and re-layouts  8.93 us
    reduce_sum x1, other arithmetic, per_device(): jnp.sum(v * after[None, None], axis=2)  6.89 us
    ppermute x2, starting transfers between devices, padded(): lax.ppermute(lax.slice_in_dim(block, block.shape[dim] - width, None, axis...  6.58 us
    ppermute x2, starting transfers between devices, padded(): lax.ppermute(lax.slice_in_dim(block, 0, width, axis=dim), axis, backward)  6.33 us
    pallas_call x1, Pallas kernels, per_device(): pl.pallas_call(reduced_kernel, out_shape=whole((parts, 10, chunk)), in_sp...  5.36 us
  transfers between devices with their start and end apart: 5, of which 0 were waited for; matrix products, arithmetic and copies ran while one was open for 19% of the time, Pallas kernels for 0%

profile of v1, /device:TPU:1, one launch (start us, length us, event | category | flops | bytes accessed | tf_op | source)
XLA Modules:
  0.0 110.5 jit_solution(15166069747809647717)
XLA Ops:
  0.0 1.0 fusion.8
  1.0 1.3 %collective-permute-start = (f32[1,5,1024]{2,0,1:T(1,128)S(1)}, f32[1,5,1024]{2,0,1:T(1,128)S(1)}, u32[]{:S(2)}, u32[]{:S(2)}) collective-permute-start(f32[1,5,1024]{2,0,1:T(1,128)S(1)} %get-tuple-element.9), channel_id=1, source_target_pairs={{16,0},{32,16},{48,32},{64,48},{80,64},{96,80},{112,96},{128,112},... | collective-permute-start | bytes 61448 | tf_op jit(solution)/shard_map/ppermute | solution.py:20
  2.3 4.7 %collective-permute-start.1 = (f32[1,5,1024]{2,0,1:T(1,128)S(1)}, f32[1,5,1024]{2,0,1:T(1,128)S(1)}, u32[]{:S(2)}, u32[]{:S(2)}) collective-permute-start(f32[1,5,1024]{2,0,1:T(1,128)S(1)} %get-tuple-element.10), channel_id=1, source_target_pairs={{0,16},{16,32},{32,48},{48,64},{64,80},{80,96},{96,112},{112,128},... | collective-permute-start | bytes 61448 | tf_op jit(solution)/shard_map/ppermute | solution.py:17
  7.0 1.1 fusion.9
  8.1 5.0 %collective-permute-start.2 = (f32[64,5,1]{2,0,1:T(8,128)S(1)}, f32[64,5,1]{2,0,1:T(8,128)S(1)}, u32[]{:S(2)}, u32[]{:S(2)}) collective-permute-start(f32[64,5,1]{2,0,1:T(8,128)S(1)} %get-tuple-element.11), channel_id=1, source_target_pairs={{1,0},{2,1},{3,2},{4,3},{5,4},{6,5},{7,6},{8,7},{9,8},{10,9},{11,1... | collective-permute-start | bytes 3848 | tf_op jit(solution)/shard_map/ppermute | solution.py:20
  13.1 1.9 %collective-permute-start.3 = (f32[64,5,1]{2,0,1:T(8,128)S(1)}, f32[64,5,1]{2,0,1:T(8,128)S(1)}, u32[]{:S(2)}, u32[]{:S(2)}) collective-permute-start(f32[64,5,1]{2,0,1:T(8,128)S(1)} %get-tuple-element.12), channel_id=1, source_target_pairs={{0,1},{1,2},{2,3},{3,4},{4,5},{5,6},{6,7},{7,8},{8,9},{9,10},{10,1... | collective-permute-start | bytes 3848 | tf_op jit(solution)/shard_map/ppermute | solution.py:17
  15.1 1.7 %copy.26 = f32[8,8,8,128]{3,2,1,0:T(8,128)} copy(f32[8,8,8,128]{3,1,2,0:T(8,128)} %bitcast.40) | data formatting | bytes 524288
  16.8 4.5 %copy.27 = f32[200,8,8,128]{3,2,1,0:T(8,128)S(1)} copy(f32[200,8,8,128]{3,1,2,0:T(8,128)} %bitcast.32) | data formatting | bytes 13107200
  21.3 0.0 copy-start
  21.3 0.0 copy-start.1
  21.3 3.1 %copy.16.jac_ref = f32[64,25,8,128]{3,2,1,0:T(8,128)} copy(f32[64,25,8,128]{3,2,0,1:T(8,128)S(1)} %bitcast.31) | data formatting | bytes 13107200 | tf_op jit(solution)/shard_map/reshape | solution.py:190
  24.3 0.0 collective-permute-done.2
  24.3 0.0 collective-permute-done.3
  24.4 0.0 collective-permute-done
  24.4 0.0 collective-permute-done.1
  24.4 0.0 copy-done
  24.4 0.0 copy-done.1
  24.4 0.8 fusion.3
  25.2 0.3 copy.28
  25.5 1.1 %copy.17.src_ref = f32[64,5,8,128]{3,2,1,0:T(8,128)} copy(f32[64,5,8,128]{3,2,0,1:T(8,128)S(1)} %bitcast.34) | data formatting | bytes 2621440 | tf_op jit(solution)/shard_map/reshape | solution.py:189
  26.6 26.0 %shard_map.46 = f32[64,55,8,128]{3,2,1,0:T(8,128)} custom-call(f32[64,8,128]{2,1,0:T(8,128)} %bitcast.38, f32[64,25,8,128]{3,2,1,0:T(8,128)} %copy.16.jac_ref, f32[64,5,8,128]{3,2,1,0:T(8,128)} %copy.17.src_ref), custom_call_target="tpu_custom_call" | custom-call | tf_op jit(solution)/shard_map/pallas_call | solution.py:193
  52.6 1.1 fusion.7
  53.7 0.2 all_to_all.15
  53.9 0.4 copy.18
  54.3 19.7 %all_to_all.21 = f32[110,16,64]{0,2,1:T(8,128)S(1)} all-to-all(f32[110,16,64]{0,2,1:T(8,128)S(1)} %copy.18), channel_id=1, replica_groups=mesh['line'=16,'plane'=16] {'line'}, dimensions={1} | all-to-all | bytes 901120 | tf_op jit(solution)/shard_map/all_to_all | solution.py:203
  74.1 0.6 reshape.38
  74.7 1.1 %fusion.10 = (f32[16,1,55,64]{2,1,3,0:T(1,128)S(1)}, f32[16,1,55,64]{2,1,3,0:T(1,128)S(1)}) fusion(f32[16,2,55,64]{2,1,3,0:T(2,128)S(1)} %reshape.38), kind=kLoop, calls=%fused_computation.18 | loop fusion | bytes 901120 | tf_op jit(solution)/shard_map/slice | solution.py:206
  75.8 0.4 copy.25
  76.2 0.4 copy.24
  76.6 0.8 concatenate.25.head_ref
  77.4 0.8 concatenate.24.tail_ref
  78.2 5.4 %shard_map.47 = f32[16,10,64]{2,1,0:T(8,128)} custom-call(f32[17,55,64]{2,1,0:T(8,128)} %concatenate.24.tail_ref, f32[17,55,64]{2,1,0:T(8,128)} %concatenate.25.head_ref), custom_call_target="tpu_custom_call" | custom-call | tf_op jit(solution)/shard_map/pallas_call | solution.py:207
  83.6 1.6 %reshape.41 = f32[16,1,640]{2,1,0:T(1,128)} reshape(f32[16,10,64]{2,1,0:T(8,128)} %shard_map.47) | data formatting | bytes 81920
  85.2 3.5 %all-to-all-start.1 = ((f32[16,1,640]{2,1,0:T(1,128)}), f32[16,1,640]{2,1,0:T(1,128)S(1)}, u32[]{:S(2)}, u32[]{:S(2)}) async-start(f32[16,1,640]{2,1,0:T(1,128)} %reshape.41), calls=%async_computation.1 | async-start | bytes 81920 | tf_op jit(solution)/shard_map/all_to_all | solution.py:214
  88.7 10.4 %fusion.6 = (f32[64,25,8,128]{3,2,1,0:T(8,128)}, f32[64,25,8,128]{3,2,1,0:T(8,128)}) fusion(f32[64,55,8,128]{3,2,1,0:T(8,128)} %shard_map.46), kind=kLoop, calls=%fused_computation.14 | loop fusion | bytes 26214400 | tf_op jit(solution)/shard_map/slice | solution.py:219
  99.1 0.0 all-to-all-done.1
  99.1 0.5 broadcast.4
  99.6 0.7 reduce
  100.4 0.1 reshape.42
  100.5 0.1 mul.36
  100.6 0.1 mul.39
  100.7 6.9 %multiply_reduce_fusion = (f32[64,5,8,128]{3,2,1,0:T(8,128)S(1)}, f32[64,5,8,128]{3,2,1,0:T(8,128)S(1)}) fusion(f32[64,5,5,8,128]{4,3,2,1,0:T(8,128)} %bitcast.30, f32[5,8,128]{2,1,0:T(8,128)S(1)} %mul.39, f32[64,5,5,8,128]{4,3,2,1,0:T(8,128)} %bitcast.29, f32[5,8,128]{2,1,0:T(8,128)S(1)} %mul.36), kind=kLoop, calls=%fused_computation | loop fusion | flops 5898240 | bytes 15769600 | tf_op jit(solution)/shard_map/reduce_sum | solution.py:221
  107.6 1.6 %fusion = f32[64,5,8,128]{3,2,1,0:T(8,128)S(1)} fusion(f32[64,5,8,128]{3,2,1,0:T(8,128)S(1)} %get-tuple-element.17, f32[64,5,8,128]{3,2,1,0:T(8,128)S(1)} %get-tuple-element.18, f32[64,55,8,128]{3,2,1,0:T(8,128)} %shard_map.46), kind=kLoop, calls=%fused_computation.3 | loop fusion | flops 655360 | bytes 5242880 | tf_op jit(solution)/shard_map/sub | solution.py:221
  109.1 0.1 copy.23
  109.2 1.3 %reshape.40 = f32[64,5,1024]{2,0,1:T(8,128)} reshape(f32[64,5,8,128]{3,2,0,1:T(8,128)S(1)} %copy.23) | data formatting | bytes 2621440 | tf_op jit(solution)/shard_map/reshape | solution.py:222
  (4 shorter events, 0.1 us)
Async XLA Ops:
  1.0 23.3 %collective-permute-start = (f32[1,5,1024]{2,0,1:T(1,128)S(1)}, f32[1,5,1024]{2,0,1:T(1,128)S(1)}, u32[]{:S(2)}, u32[]{:S(2)}) collective-permute-start(f32[1,5,1024]{2,0,1:T(1,128)S(1)} %get-tuple-element.9), channel_id=1, source_target_pairs={{16,0},{32,16},{48,32},{64,48},{80,64},{96,80},{112,96},{128,112},... | collective-permute-start | bytes 61448 | tf_op jit(solution)/shard_map/ppermute | solution.py:20
  2.3 22.0 %collective-permute-start.1 = (f32[1,5,1024]{2,0,1:T(1,128)S(1)}, f32[1,5,1024]{2,0,1:T(1,128)S(1)}, u32[]{:S(2)}, u32[]{:S(2)}) collective-permute-start(f32[1,5,1024]{2,0,1:T(1,128)S(1)} %get-tuple-element.10), channel_id=1, source_target_pairs={{0,16},{16,32},{32,48},{48,64},{64,80},{80,96},{96,112},{112,128},... | collective-permute-start | bytes 61448 | tf_op jit(solution)/shard_map/ppermute | solution.py:17
  8.1 16.2 %collective-permute-start.2 = (f32[64,5,1]{2,0,1:T(8,128)S(1)}, f32[64,5,1]{2,0,1:T(8,128)S(1)}, u32[]{:S(2)}, u32[]{:S(2)}) collective-permute-start(f32[64,5,1]{2,0,1:T(8,128)S(1)} %get-tuple-element.11), channel_id=1, source_target_pairs={{1,0},{2,1},{3,2},{4,3},{5,4},{6,5},{7,6},{8,7},{9,8},{10,9},{11,1... | collective-permute-start | bytes 3848 | tf_op jit(solution)/shard_map/ppermute | solution.py:20
  13.1 11.2 %collective-permute-start.3 = (f32[64,5,1]{2,0,1:T(8,128)S(1)}, f32[64,5,1]{2,0,1:T(8,128)S(1)}, u32[]{:S(2)}, u32[]{:S(2)}) collective-permute-start(f32[64,5,1]{2,0,1:T(8,128)S(1)} %get-tuple-element.12), channel_id=1, source_target_pairs={{0,1},{1,2},{2,3},{3,4},{4,5},{5,6},{6,7},{7,8},{8,9},{9,10},{10,1... | collective-permute-start | bytes 3848 | tf_op jit(solution)/shard_map/ppermute | solution.py:17
  21.3 3.1 %copy-start = (f32[64,5,1024]{2,0,1:T(8,128)S(1)}, f32[64,5,1024]{2,0,1:T(8,128)}, u32[]{:S(2)}) copy-start(f32[64,5,1024]{2,0,1:T(8,128)} %param.5) | copy-start | bytes 3932164
  21.3 3.1 %copy-start.1 = (f32[64,5,1024]{2,0,1:T(8,128)S(1)}, f32[64,5,1024]{2,0,1:T(8,128)}, u32[]{:S(2)}) copy-start(f32[64,5,1024]{2,0,1:T(8,128)} %param.4) | copy-start | bytes 3932164
  85.2 13.9 %all-to-all-start.1 = ((f32[16,1,640]{2,1,0:T(1,128)}), f32[16,1,640]{2,1,0:T(1,128)S(1)}, u32[]{:S(2)}, u32[]{:S(2)}) async-start(f32[16,1,640]{2,1,0:T(1,128)} %reshape.41), calls=%async_computation.1 | async-start | bytes 81920 | tf_op jit(solution)/shard_map/all_to_all | solution.py:214

commit v2 on v1

--- a/solution.py
+++ b/solution.py
@@ -63,8 +63,9 @@
 
 
 def factor_kernel(vis_ref, jac_ref, src_ref, out_ref):
-    cells = vis_ref.shape[0]
-    tile = vis_ref.shape[1:]
+    cells = out_ref.shape[0]
+    tile = out_ref.shape[2:]
+    rows = tile[0]
     zero = jnp.zeros(tile, jnp.float32)
     one = jnp.ones(tile, jnp.float32)
 
@@ -72,8 +73,10 @@
         c_prev = grid_of(carry[0:25], NV, NV)
         g_prev = [[x] for x in carry[25:30]]
         w_prev = grid_of(carry[30:55], NV, NV)
-        spread = vis_ref[i]
-        jac = [[jac_ref[i, a * NV + b] for b in range(NV)] for a in range(NV)]
+        block = i // 8
+        picked = pl.ds(i % 8, rows, stride=8)
+        spread = vis_ref[block, picked, :]
+        jac = [[jac_ref[a * NV + b, block, picked, :] for b in range(NV)] for a in range(NV)]
         lower = [[(-spread - jac[a][b]) if a == b else (-jac[a][b]) for b in range(NV)] for a in range(NV)]
         upper = [[(-spread + jac[a][b]) if a == b else jac[a][b] for b in range(NV)] for a in range(NV)]
         centre = 1.0 + 2.0 * spread
@@ -83,7 +86,7 @@
         lw = matmul(lower, w_prev, NV, NV, NV)
         cols = []
         for a in range(NV):
-            cols.append(upper[a] + [src_ref[i, a] - lg[a][0]] + [-x for x in lw[a]])
+            cols.append(upper[a] + [src_ref[a, block, picked, :] - lg[a][0]] + [-x for x in lw[a]])
         sol = gauss_jordan(schur, cols)
         c_new = [row[0:NV] for row in sol]
         g_new = [row[NV] for row in sol]
@@ -115,47 +118,60 @@
     lax.fori_loop(0, cells, backward, tuple(init))
 
 
-def reduced_kernel(tail_ref, head_ref, out_ref, keep_ref):
-    steps = tail_ref.shape[0]
-    lanes = tail_ref.shape[2]
-
-    def row(ref, q, k):
-        return ref[q, k:k + 1, :]
-
-    def forward(q, carry):
-        x_prev = grid_of(carry[0:25], NV, NV)
-        u_prev = [[x] for x in carry[25:30]]
-        y63 = [row(tail_ref, q, a) for a in range(NV)]
-        w63 = [[row(tail_ref, q, 5 + a * NV + b) for b in range(NV)] for a in range(NV)]
-        v63 = [[row(tail_ref, q, 30 + a * NV + b) for b in range(NV)] for a in range(NV)]
-        y0 = [row(head_ref, q, a) for a in range(NV)]
-        w0 = [[row(head_ref, q, 5 + a * NV + b) for b in range(NV)] for a in range(NV)]
-        v0 = [[row(head_ref, q, 30 + a * NV + b) for b in range(NV)] for a in range(NV)]
-        wx = matmul(w63, x_prev, NV, NV, NV)
-        m = [[v63[a][b] - wx[a][b] for b in range(NV)] for a in range(NV)]
-        wu = matmul(w63, u_prev, NV, NV, 1)
-        av = [[y63[a] - wu[a][0]] for a in range(NV)]
-        wm = matmul(w0, m, NV, NV, NV)
-        k_mat = [[(1.0 - wm[a][b]) if a == b else (-wm[a][b]) for b in range(NV)] for a in range(NV)]
-        wa = matmul(w0, av, NV, NV, 1)
-        cols = [v0[a] + [y0[a] - wa[a][0]] for a in range(NV)]
-        sol = gauss_jordan(k_mat, cols)
-        y_new = [r[0:NV] for r in sol]
-        v_new = [[r[NV]] for r in sol]
-        my = matmul(m, y_new, NV, NV, NV)
-        x_new = [[-my[a][b] for b in range(NV)] for a in range(NV)]
-        mv = matmul(m, v_new, NV, NV, 1)
-        u_new = [av[a][0] - mv[a][0] for a in range(NV)]
-        flat = flat_of(x_new) + flat_of(y_new) + u_new + [r[0] for r in v_new]
+def interface_step(tail, head, carry):
+    x_prev = grid_of(carry[0:25], NV, NV)
+    u_prev = [[x] for x in carry[25:30]]
+    y63 = tail[0:5]
+    w63 = grid_of(tail[5:30], NV, NV)
+    v63 = grid_of(tail[30:55], NV, NV)
+    y0 = head[0:5]
+    w0 = grid_of(head[5:30], NV, NV)
+    v0 = grid_of(head[30:55], NV, NV)
+    wx = matmul(w63, x_prev, NV, NV, NV)
+    m = [[v63[a][b] - wx[a][b] for b in range(NV)] for a in range(NV)]
+    wu = matmul(w63, u_prev, NV, NV, 1)
+    av = [[y63[a] - wu[a][0]] for a in range(NV)]
+    wm = matmul(w0, m, NV, NV, NV)
+    k_mat = [[(1.0 - wm[a][b]) if a == b else (-wm[a][b]) for b in range(NV)] for a in range(NV)]
+    wa = matmul(w0, av, NV, NV, 1)
+    cols = [v0[a] + [y0[a] - wa[a][0]] for a in range(NV)]
+    sol = gauss_jordan(k_mat, cols)
+    y_new = [r[0:NV] for r in sol]
+    v_new = [[r[NV]] for r in sol]
+    my = matmul(m, y_new, NV, NV, NV)
+    x_new = [[-my[a][b] for b in range(NV)] for a in range(NV)]
+    mv = matmul(m, v_new, NV, NV, 1)
+    u_new = [av[a][0] - mv[a][0] for a in range(NV)]
+    flat = flat_of(x_new) + flat_of(y_new) + u_new + [r[0] for r in v_new]
+    return flat, tuple(flat[0:25] + u_new)
+
+
+def reduced_kernel(ends_ref, out_ref, keep_ref):
+    parts = ends_ref.shape[0]
+    lanes = ends_ref.shape[2]
+    zero = jnp.zeros((1, lanes), jnp.float32)
+
+    def rows_of(p, first):
+        return [ends_ref[p, first + k:first + k + 1, :] for k in range(55)]
+
+    def keep(q, flat):
         for k in range(60):
             keep_ref[q, k:k + 1, :] = flat[k]
-        return tuple(flat[0:25] + u_new)
-
-    zero = jnp.zeros((1, lanes), jnp.float32)
-    lax.fori_loop(0, steps, forward, tuple([zero] * 30))
+
+    flat, carry = interface_step([zero] * 55, rows_of(0, 0), tuple([zero] * 30))
+    keep(0, flat)
+
+    def forward(q, carry):
+        flat, carry = interface_step(rows_of(q - 1, 55), rows_of(q, 0), carry)
+        keep(q, flat)
+        return carry
+
+    carry = lax.fori_loop(1, parts, forward, carry)
+    flat, carry = interface_step(rows_of(parts - 1, 55), [zero] * 55, carry)
+    keep(parts, flat)
 
     h_next = [[zero] for _ in range(NV)]
-    for q in range(steps - 1, -1, -1):
+    for q in range(parts, -1, -1):
         x_q = [[keep_ref[q, a * NV + b:a * NV + b + 1, :] for b in range(NV)] for a in range(NV)]
         y_q = [[keep_ref[q, 25 + a * NV + b:26 + a * NV + b, :] for b in range(NV)] for a in range(NV)]
         u_q = [keep_ref[q, 50 + a:51 + a, :] for a in range(NV)]
@@ -164,7 +180,7 @@
         yh = matmul(y_q, h_next, NV, NV, 1)
         t_prev = [u_q[a] - xh[a][0] for a in range(NV)]
         h_here = [v_q[a] - yh[a][0] for a in range(NV)]
-        if q <= steps - 2:
+        if q <= parts - 1:
             for a in range(NV):
                 out_ref[q, a:a + 1, :] = t_prev[a]
         if q >= 1:
@@ -173,22 +189,44 @@
         h_next = [[x] for x in h_here]
 
 
+def combine_kernel(fac_ref, bnd_ref, out_ref):
+    rows = fac_ref.shape[2]
+    before = [bnd_ref[b] for b in range(NV)]
+    after = [bnd_ref[NV + b] for b in range(NV)]
+    for c in range(fac_ref.shape[0]):
+        for a in range(NV):
+            w_t = fac_ref[c, 5 + a * NV] * before[0]
+            v_h = fac_ref[c, 30 + a * NV] * after[0]
+            for b in range(1, NV):
+                w_t = w_t + fac_ref[c, 5 + a * NV + b] * before[b]
+                v_h = v_h + fac_ref[c, 30 + a * NV + b] * after[b]
+            out_ref[a, 0, pl.ds(c, rows, stride=8), :] = fac_ref[c, a] - w_t - v_h
+
+
 def whole(shape):
     return jax.ShapeDtypeStruct(shape, jnp.float32)
+
+
+def stored_order(array, lead):
+    *head, cells, lines = array.shape
+    rows = lines // 128
+    split = array.reshape(*head, cells // 8, 8, rows, 128)
+    return jnp.swapaxes(split, -3, -2).reshape(*head, cells // 8, rows * 8, 128)
 
 
 def per_device(flux_x, flux_z, viscous, jacobian):
     cells, line_count = viscous.shape
     rows = line_count // 128
     parts = lax.axis_size("line")
+    chunk = line_count // parts
     stream = padded(flux_x, (("line", 0),), 1)
     across = padded(flux_z, (("plane", 2),), 1)
     source = -0.5 * courant * (stream[2:] - stream[:-2]) - 0.5 * courant * (
         across[:, :, 2:] - across[:, :, :-2]
     )
-    src4 = source.reshape(cells, NV, rows, 128)
-    jac4 = jacobian.reshape(cells, NV * NV, rows, 128)
-    vis3 = viscous.reshape(cells, rows, 128)
+    src_s = stored_order(jnp.transpose(source, (1, 0, 2)), 1)
+    jac_s = stored_order(jnp.transpose(jacobian, (1, 2, 0, 3)).reshape(NV * NV, cells, line_count), 1)
+    vis_s = stored_order(viscous, 0)
     vmem = pl.BlockSpec(memory_space=pltpu.VMEM)
     factors = pl.pallas_call(
         factor_kernel,
@@ -196,30 +234,33 @@
         in_specs=[vmem, vmem, vmem],
         out_specs=vmem,
         compiler_params=pltpu.CompilerParams(vmem_limit_bytes=60 * 1024 * 1024),
-    )(vis3, jac4, src4)
-
-    ends = jnp.stack([factors[0], factors[cells - 1]]).reshape(2 * 55, line_count)
-    chunk = line_count // parts
-    gathered = lax.all_to_all(ends, "line", 1, 0, tiled=True).reshape(parts, 2, 55, chunk)
-    empty = jnp.zeros((1, 55, chunk), jnp.float32)
-    tails = jnp.concatenate([empty, gathered[:, 1]], 0)
-    heads = jnp.concatenate([gathered[:, 0], empty], 0)
+    )(vis_s, jac_s, src_s)
+
+    ends = jnp.stack([factors[0], factors[cells - 1]]).reshape(2 * 55, parts, chunk)
+    sent = jnp.transpose(ends, (1, 0, 2))
+    gathered = lax.all_to_all(sent, "line", 0, 0, tiled=True)
     answers = pl.pallas_call(
         reduced_kernel,
         out_shape=whole((parts, 10, chunk)),
-        in_specs=[vmem, vmem],
+        in_specs=[vmem],
         out_specs=vmem,
         scratch_shapes=[pltpu.VMEM((parts + 1, 60, chunk), jnp.float32)],
-    )(tails, heads)
+    )(gathered)
     back = lax.all_to_all(answers, "line", 0, 0, tiled=True)
-    bounds = jnp.moveaxis(back, 0, 1).reshape(10, rows, 128)
-    before = bounds[0:NV]
-    after = bounds[NV:]
-    local = factors[:, 0:NV]
-    w = factors[:, 5:30].reshape(cells, NV, NV, rows, 128)
-    v = factors[:, 30:55].reshape(cells, NV, NV, rows, 128)
-    delta = local - jnp.sum(w * before[None, None], axis=2) - jnp.sum(v * after[None, None], axis=2)
-    return delta.reshape(cells, NV, line_count)
+    bounds = jnp.moveaxis(back, 1, 0).reshape(10, rows, 128)
+    blocks = cells // 8
+    delta_s = pl.pallas_call(
+        combine_kernel,
+        out_shape=whole((NV, blocks, rows * 8, 128)),
+        grid=(blocks,),
+        in_specs=[
+            pl.BlockSpec((8, 55, rows, 128), lambda c: (c, 0, 0, 0)),
+            pl.BlockSpec((10, rows, 128), lambda c: (0, 0, 0)),
+        ],
+        out_specs=pl.BlockSpec((NV, 1, rows * 8, 128), lambda c: (0, c, 0, 0)),
+    )(factors, bounds)
+    delta = jnp.swapaxes(delta_s.reshape(NV, blocks, rows, 8, 128), 2, 3).reshape(NV, cells, line_count)
+    return jnp.transpose(delta, (1, 0, 2))
 
 
 def solution(mesh):

time: 111 us -> 100 us (0.901)
  the two profiles are of different devices: /device:TPU:1 before, /device:TPU:96 now
where the time goes in v2:
time: 100 us; the launch traced here: 99.7 us
  Pallas kernels  40.4 us (40%)
  blocking collectives  32.2 us (32%)
  starting transfers between devices  10.2 us (10%)
  local copies, waits for them, and re-layouts  7.4 us (7%)
  other arithmetic  5.22 us (5%)
  waiting for transfers between devices  4.23 us (4%)
    pallas_call x1, Pallas kernels, per_device(): pl.pallas_call(factor_kernel, out_shape=whole((cells, 55, rows, 128)), in...  26.8 us
    all_to_all x1, blocking collectives, per_device(): gathered = lax.all_to_all(sent, 'line', 0, 0, tiled=True)  21.2 us
    all_to_all x1, blocking collectives, per_device(): back = lax.all_to_all(answers, 'line', 0, 0, tiled=True)  11 us
    pallas_call x1, Pallas kernels, per_device(): pl.pallas_call(combine_kernel, out_shape=whole((NV, blocks, rows * 8, 128...  8.35 us
    ppermute x2, starting transfers between devices, padded(): lax.ppermute(lax.slice_in_dim(block, block.shape[dim] - width, None, axis...  6.95 us
    pallas_call x1, Pallas kernels, per_device(): pl.pallas_call(reduced_kernel, out_shape=whole((parts, 10, chunk)), in_sp...  5.25 us
    reshape x1, other arithmetic, stored_order(): return jnp.swapaxes(split, -3, -2).reshape(*head, cells // 8, rows * 8, 128)  4.45 us
    ppermute x2, waiting for transfers between devices, padded(): lax.ppermute(lax.slice_in_dim(block, block.shape[dim] - width, None, axis...  3.82 us
  transfers between devices with their start and end apart: 4, of which 2 were waited for; matrix products, arithmetic and copies ran while one was open for 1% of the time, Pallas kernels for 0%

profile of v2, /device:TPU:96, one launch (start us, length us, event | category | flops | bytes accessed | tf_op | source)
XLA Modules:
  0.0 99.7 jit_solution(10483809173905352832)
XLA Ops:
  0.0 1.0 %fusion.7 = (f32[1,5,1024]{2,0,1:T(1,128)S(1)}, f32[1,5,1024]{2,0,1:T(1,128)S(1)}) fusion(f32[64,5,1024]{2,0,1:T(8,128)} %param.4), kind=kLoop, calls=%fused_computation.12 | loop fusion | bytes 81920 | tf_op jit(solution)/shard_map/slice | solution.py:20
  1.0 1.3 %collective-permute-start = (f32[1,5,1024]{2,0,1:T(1,128)S(1)}, f32[1,5,1024]{2,0,1:T(1,128)S(1)}, u32[]{:S(2)}, u32[]{:S(2)}) collective-permute-start(f32[1,5,1024]{2,0,1:T(1,128)S(1)} %get-tuple-element.7), channel_id=1, source_target_pairs={{16,0},{32,16},{48,32},{64,48},{80,64},{96,80},{112,96},{128,112},... | collective-permute-start | bytes 61448 | tf_op jit(solution)/shard_map/ppermute | solution.py:20
  2.3 4.5 %collective-permute-start.1 = (f32[1,5,1024]{2,0,1:T(1,128)S(1)}, f32[1,5,1024]{2,0,1:T(1,128)S(1)}, u32[]{:S(2)}, u32[]{:S(2)}) collective-permute-start(f32[1,5,1024]{2,0,1:T(1,128)S(1)} %get-tuple-element.8), channel_id=1, source_target_pairs={{0,16},{16,32},{32,48},{48,64},{64,80},{80,96},{96,112},{112,128},... | collective-permute-start | bytes 61448 | tf_op jit(solution)/shard_map/ppermute | solution.py:17
  6.9 1.1 %fusion.8 = (f32[64,5,1]{2,0,1:T(8,128)S(1)}, f32[64,5,1]{2,0,1:T(8,128)S(1)}) fusion(f32[64,5,1024]{2,0,1:T(8,128)} %param.5), kind=kLoop, calls=%fused_computation.13 | loop fusion | bytes 5120 | tf_op jit(solution)/shard_map/slice | solution.py:20
  8.0 1.9 %collective-permute-start.2 = (f32[64,5,1]{2,0,1:T(8,128)S(1)}, f32[64,5,1]{2,0,1:T(8,128)S(1)}, u32[]{:S(2)}, u32[]{:S(2)}) collective-permute-start(f32[64,5,1]{2,0,1:T(8,128)S(1)} %get-tuple-element.9), channel_id=1, source_target_pairs={{1,0},{2,1},{3,2},{4,3},{5,4},{6,5},{7,6},{8,7},{9,8},{10,9},{11,1... | collective-permute-start | bytes 3848 | tf_op jit(solution)/shard_map/ppermute | solution.py:20
  9.9 2.4 %collective-permute-start.3 = (f32[64,5,1]{2,0,1:T(8,128)S(1)}, f32[64,5,1]{2,0,1:T(8,128)S(1)}, u32[]{:S(2)}, u32[]{:S(2)}) collective-permute-start(f32[64,5,1]{2,0,1:T(8,128)S(1)} %get-tuple-element.10), channel_id=1, source_target_pairs={{0,1},{1,2},{2,3},{3,4},{4,5},{5,6},{6,7},{7,8},{8,9},{9,10},{10,1... | collective-permute-start | bytes 3848 | tf_op jit(solution)/shard_map/ppermute | solution.py:17
  12.3 0.4 collective-permute-done.2
  12.7 3.8 %collective-permute-done.3 = f32[64,5,1]{2,0,1:T(8,128)S(1)} collective-permute-done((f32[64,5,1]{2,0,1:T(8,128)S(1)}, f32[64,5,1]{2,0,1:T(8,128)S(1)}, u32[]{:S(2)}, u32[]{:S(2)}) %collective-permute-start.3) | collective-permute-done | bytes 1312 | tf_op jit(solution)/shard_map/ppermute | solution.py:17
  16.6 0.0 collective-permute-done
  16.6 0.0 collective-permute-done.1
  16.6 4.5 %fusion.3.src_ref = f32[5,8,64,128]{3,2,1,0:T(8,128)} fusion(f32[64,5,1024]{2,0,1:T(8,128)} %param.5, f32[64,5,1]{2,0,1:T(8,128)S(1)} %collective-permute-done.3, f32[64,5,1]{2,0,1:T(8,128)S(1)} %collective-permute-done.2, f32[64,5,1024]{2,0,1:T(8,128)} %param.4, f32[1,5,1024]{2,0,1:T(1,128)S(1)} %collective-permute-done.1, ...), kind=kLoop, calls=%fused_computation.4 | loop fusion | flops 2949120 | bytes 3975680 | tf_op jit(solution)/shard_map/reshape | solution.py:214
  21.0 26.8 %shard_map.46.fac_ref = f32[64,55,8,128]{3,2,1,0:T(8,128)} custom-call(f32[8,64,128]{2,1,0:T(8,128)} %bitcast.34, f32[25,8,64,128]{3,2,1,0:T(8,128)} %bitcast.31, f32[5,8,64,128]{3,2,1,0:T(8,128)} %fusion.3.src_ref), custom_call_target="tpu_custom_call" | custom-call | tf_op jit(solution)/shard_map/pallas_call | solution.py:231
  47.8 1.1 %fusion.6 = (f32[1,55,8,128]{3,2,1,0:T(8,128)S(1)}, f32[1,55,8,128]{3,2,1,0:T(8,128)S(1)}) fusion(f32[64,55,8,128]{3,2,1,0:T(8,128)} %shard_map.46.fac_ref), kind=kLoop, calls=%fused_computation.11 | loop fusion | bytes 901120 | tf_op jit(solution)/shard_map/slice | solution.py:239
  48.9 0.2 reshape.32
  49.1 0.4 copy.8
  49.5 21.2 %all_to_all.10 = f32[16,110,64]{1,2,0:T(8,128)S(1)} all-to-all(f32[16,110,64]{1,2,0:T(8,128)S(1)} %copy.8), channel_id=1, replica_groups=mesh['line'=16,'plane'=16] {'line'}, dimensions={0} | all-to-all | bytes 901120 | tf_op jit(solution)/shard_map/all_to_all | solution.py:241
  70.7 1.3 %copy.9.ends_ref = f32[16,110,64]{2,1,0:T(8,128)} copy(f32[16,110,64]{1,2,0:T(8,128)S(1)} %all_to_all.10) | data formatting | bytes 901120 | tf_op jit(solution)/shard_map/all_to_all | solution.py:241
  72.0 5.3 %shard_map.47 = f32[16,10,64]{2,1,0:T(8,128)} custom-call(f32[16,110,64]{2,1,0:T(8,128)} %copy.9.ends_ref), custom_call_target="tpu_custom_call" | custom-call | tf_op jit(solution)/shard_map/pallas_call | solution.py:242
  77.2 1.0 %reshape.36 = f32[16,1,640]{2,1,0:T(1,128)S(1)} reshape(f32[16,10,64]{2,1,0:T(8,128)} %shard_map.47) | data formatting | bytes 81920
  78.3 11.0 %all_to_all.11 = f32[16,1,640]{2,1,0:T(1,128)S(1)} all-to-all(f32[16,1,640]{2,1,0:T(1,128)S(1)} %reshape.36), channel_id=1, replica_groups=mesh['line'=16,'plane'=16] {'line'}, dimensions={0} | all-to-all | bytes 81920 | tf_op jit(solution)/shard_map/all_to_all | solution.py:249
  89.2 0.5 broadcast
  89.7 0.7 reduce
  90.5 0.1 reshape.37
  90.6 0.7 reshape.33.bnd_ref
  91.3 8.3 %shard_map.48 = f32[5,8,64,128]{3,2,1,0:T(8,128)} custom-call(f32[64,55,8,128]{3,2,1,0:T(8,128)} %shard_map.46.fac_ref, f32[10,8,128]{2,1,0:T(8,128)} %reshape.33.bnd_ref), custom_call_target="tpu_custom_call" | custom-call | tf_op jit(solution)/shard_map/pallas_call | solution.py:252
  (2 shorter events, 0.1 us)
Async XLA Ops:
  1.0 15.5 %collective-permute-start = (f32[1,5,1024]{2,0,1:T(1,128)S(1)}, f32[1,5,1024]{2,0,1:T(1,128)S(1)}, u32[]{:S(2)}, u32[]{:S(2)}) collective-permute-start(f32[1,5,1024]{2,0,1:T(1,128)S(1)} %get-tuple-element.7), channel_id=1, source_target_pairs={{16,0},{32,16},{48,32},{64,48},{80,64},{96,80},{112,96},{128,112},... | collective-permute-start | bytes 61448 | tf_op jit(solution)/shard_map/ppermute | solution.py:20
  2.3 14.2 %collective-permute-start.1 = (f32[1,5,1024]{2,0,1:T(1,128)S(1)}, f32[1,5,1024]{2,0,1:T(1,128)S(1)}, u32[]{:S(2)}, u32[]{:S(2)}) collective-permute-start(f32[1,5,1024]{2,0,1:T(1,128)S(1)} %get-tuple-element.8), channel_id=1, source_target_pairs={{0,16},{16,32},{32,48},{48,64},{64,80},{80,96},{96,112},{112,128},... | collective-permute-start | bytes 61448 | tf_op jit(solution)/shard_map/ppermute | solution.py:17
  8.0 4.7 %collective-permute-start.2 = (f32[64,5,1]{2,0,1:T(8,128)S(1)}, f32[64,5,1]{2,0,1:T(8,128)S(1)}, u32[]{:S(2)}, u32[]{:S(2)}) collective-permute-start(f32[64,5,1]{2,0,1:T(8,128)S(1)} %get-tuple-element.9), channel_id=1, source_target_pairs={{1,0},{2,1},{3,2},{4,3},{5,4},{6,5},{7,6},{8,7},{9,8},{10,9},{11,1... | collective-permute-start | bytes 3848 | tf_op jit(solution)/shard_map/ppermute | solution.py:20
  9.9 6.6 %collective-permute-start.3 = (f32[64,5,1]{2,0,1:T(8,128)S(1)}, f32[64,5,1]{2,0,1:T(8,128)S(1)}, u32[]{:S(2)}, u32[]{:S(2)}) collective-permute-start(f32[64,5,1]{2,0,1:T(8,128)S(1)} %get-tuple-element.10), channel_id=1, source_target_pairs={{0,1},{1,2},{2,3},{3,4},{4,5},{5,6},{6,7},{7,8},{8,9},{9,10},{10,1... | collective-permute-start | bytes 3848 | tf_op jit(solution)/shard_map/ppermute | solution.py:17

commit v3 on v2

--- a/solution.py
+++ b/solution.py
@@ -62,14 +62,34 @@
     return [x for row in grid for x in row]
 
 
-def factor_kernel(vis_ref, jac_ref, src_ref, out_ref):
+def factor_kernel(vis_hbm, jac_hbm, src_hbm, out_hbm, vis_ref, jac_ref, src_ref, out_ref, in_sem, out_sem):
     cells = out_ref.shape[0]
+    blocks = cells // 8
     tile = out_ref.shape[2:]
     rows = tile[0]
     zero = jnp.zeros(tile, jnp.float32)
     one = jnp.ones(tile, jnp.float32)
 
+    def arrivals(b):
+        return [
+            pltpu.make_async_copy(vis_hbm.at[b], vis_ref.at[b], in_sem.at[0, b]),
+            pltpu.make_async_copy(jac_hbm.at[:, b], jac_ref.at[:, b], in_sem.at[1, b]),
+            pltpu.make_async_copy(src_hbm.at[:, b], src_ref.at[:, b], in_sem.at[2, b]),
+        ]
+
+    def departure(b):
+        return pltpu.make_async_copy(out_ref.at[pl.ds(b * 8, 8)], out_hbm.at[pl.ds(b * 8, 8)], out_sem.at[b])
+
+    for b in range(blocks):
+        for copy in arrivals(b):
+            copy.start()
+
     def forward(i, carry):
+        @pl.when(i % 8 == 0)
+        def _():
+            for copy in arrivals(i // 8):
+                copy.wait()
+
         c_prev = grid_of(carry[0:25], NV, NV)
         g_prev = [[x] for x in carry[25:30]]
         w_prev = grid_of(carry[30:55], NV, NV)
@@ -112,10 +132,17 @@
         flat = y + flat_of(w) + flat_of(v)
         for k in range(55):
             out_ref[i, k] = flat[k]
+
+        @pl.when(i % 8 == 0)
+        def _():
+            departure(i // 8).start()
+
         return tuple(flat)
 
     init = [zero] * 30 + flat_of([[(-one if a == b else zero) for b in range(NV)] for a in range(NV)])
     lax.fori_loop(0, cells, backward, tuple(init))
+    for b in range(blocks):
+        departure(b).wait()
 
 
 def interface_step(tail, head, carry):
@@ -228,11 +255,20 @@
     jac_s = stored_order(jnp.transpose(jacobian, (1, 2, 0, 3)).reshape(NV * NV, cells, line_count), 1)
     vis_s = stored_order(viscous, 0)
     vmem = pl.BlockSpec(memory_space=pltpu.VMEM)
+    hbm = pl.BlockSpec(memory_space=pl.ANY)
     factors = pl.pallas_call(
         factor_kernel,
         out_shape=whole((cells, 55, rows, 128)),
-        in_specs=[vmem, vmem, vmem],
-        out_specs=vmem,
+        in_specs=[hbm, hbm, hbm],
+        out_specs=hbm,
+        scratch_shapes=[
+            pltpu.VMEM(vis_s.shape, jnp.float32),
+            pltpu.VMEM(jac_s.shape, jnp.float32),
+            pltpu.VMEM(src_s.shape, jnp.float32),
+            pltpu.VMEM((cells, 55, rows, 128), jnp.float32),
+            pltpu.SemaphoreType.DMA((3, cells // 8)),
+            pltpu.SemaphoreType.DMA((cells // 8,)),
+        ],
         compiler_params=pltpu.CompilerParams(vmem_limit_bytes=60 * 1024 * 1024),
     )(vis_s, jac_s, src_s)
 

time: 100 us -> 94.8 us (0.948)
  Pallas kernels: 40.4 us -> 35.2 us
    pallas_call x1, Pallas kernels: 26.8 us -> 21.6 us  [per_device(): pl.pallas_call(factor_kernel, out_shape=whole((cells, 55, rows, 128)), in...]
where the time goes in v3:
time: 94.8 us; the launch traced here: 94.4 us
  Pallas kernels  35.2 us (37%)
  blocking collectives  32.2 us (34%)
  starting transfers between devices  10.2 us (11%)
  local copies, waits for them, and re-layouts  7.4 us (8%)
  other arithmetic  5.22 us (6%)
  waiting for transfers between devices  4.23 us (4%)
    pallas_call x1, Pallas kernels, per_device(): pl.pallas_call(factor_kernel, out_shape=whole((cells, 55, rows, 128)), in...  21.6 us
    all_to_all x1, blocking collectives, per_device(): gathered = lax.all_to_all(sent, 'line', 0, 0, tiled=True)  21.2 us
    all_to_all x1, blocking collectives, per_device(): back = lax.all_to_all(answers, 'line', 0, 0, tiled=True)  11 us
    pallas_call x1, Pallas kernels, per_device(): pl.pallas_call(combine_kernel, out_shape=whole((NV, blocks, rows * 8, 128...  8.35 us
    ppermute x2, starting transfers between devices, padded(): lax.ppermute(lax.slice_in_dim(block, block.shape[dim] - width, None, axis...  6.95 us
    pallas_call x1, Pallas kernels, per_device(): pl.pallas_call(reduced_kernel, out_shape=whole((parts, 10, chunk)), in_sp...  5.25 us
    reshape x1, other arithmetic, stored_order(): return jnp.swapaxes(split, -3, -2).reshape(*head, cells // 8, rows * 8, 128)  4.45 us
    ppermute x2, waiting for transfers between devices, padded(): lax.ppermute(lax.slice_in_dim(block, block.shape[dim] - width, None, axis...  3.82 us
  transfers between devices with their start and end apart: 4, of which 2 were waited for; matrix products, arithmetic and copies ran while one was open for 1% of the time, Pallas kernels for 0%

profile of v3, /device:TPU:96, one launch (start us, length us, event | category | flops | bytes accessed | tf_op | source)
XLA Modules:
  0.0 94.4 jit_solution(2163441815960251735)
XLA Ops:
  0.0 1.0 %fusion.7 = (f32[1,5,1024]{2,0,1:T(1,128)S(1)}, f32[1,5,1024]{2,0,1:T(1,128)S(1)}) fusion(f32[64,5,1024]{2,0,1:T(8,128)} %param.4), kind=kLoop, calls=%fused_computation.12 | loop fusion | bytes 81920 | tf_op jit(solution)/shard_map/slice | solution.py:20
  1.0 1.3 %collective-permute-start = (f32[1,5,1024]{2,0,1:T(1,128)S(1)}, f32[1,5,1024]{2,0,1:T(1,128)S(1)}, u32[]{:S(2)}, u32[]{:S(2)}) collective-permute-start(f32[1,5,1024]{2,0,1:T(1,128)S(1)} %get-tuple-element.7), channel_id=1, source_target_pairs={{16,0},{32,16},{48,32},{64,48},{80,64},{96,80},{112,96},{128,112},... | collective-permute-start | bytes 61448 | tf_op jit(solution)/shard_map/ppermute | solution.py:20
  2.3 4.5 %collective-permute-start.1 = (f32[1,5,1024]{2,0,1:T(1,128)S(1)}, f32[1,5,1024]{2,0,1:T(1,128)S(1)}, u32[]{:S(2)}, u32[]{:S(2)}) collective-permute-start(f32[1,5,1024]{2,0,1:T(1,128)S(1)} %get-tuple-element.8), channel_id=1, source_target_pairs={{0,16},{16,32},{32,48},{48,64},{64,80},{80,96},{96,112},{112,128},... | collective-permute-start | bytes 61448 | tf_op jit(solution)/shard_map/ppermute | solution.py:17
  6.9 1.1 %fusion.8 = (f32[64,5,1]{2,0,1:T(8,128)S(1)}, f32[64,5,1]{2,0,1:T(8,128)S(1)}) fusion(f32[64,5,1024]{2,0,1:T(8,128)} %param.5), kind=kLoop, calls=%fused_computation.13 | loop fusion | bytes 5120 | tf_op jit(solution)/shard_map/slice | solution.py:20
  8.0 1.9 %collective-permute-start.2 = (f32[64,5,1]{2,0,1:T(8,128)S(1)}, f32[64,5,1]{2,0,1:T(8,128)S(1)}, u32[]{:S(2)}, u32[]{:S(2)}) collective-permute-start(f32[64,5,1]{2,0,1:T(8,128)S(1)} %get-tuple-element.9), channel_id=1, source_target_pairs={{1,0},{2,1},{3,2},{4,3},{5,4},{6,5},{7,6},{8,7},{9,8},{10,9},{11,1... | collective-permute-start | bytes 3848 | tf_op jit(solution)/shard_map/ppermute | solution.py:20
  9.9 2.4 %collective-permute-start.3 = (f32[64,5,1]{2,0,1:T(8,128)S(1)}, f32[64,5,1]{2,0,1:T(8,128)S(1)}, u32[]{:S(2)}, u32[]{:S(2)}) collective-permute-start(f32[64,5,1]{2,0,1:T(8,128)S(1)} %get-tuple-element.10), channel_id=1, source_target_pairs={{0,1},{1,2},{2,3},{3,4},{4,5},{5,6},{6,7},{7,8},{8,9},{9,10},{10,1... | collective-permute-start | bytes 3848 | tf_op jit(solution)/shard_map/ppermute | solution.py:17
  12.3 0.4 collective-permute-done.2
  12.7 3.8 %collective-permute-done.3 = f32[64,5,1]{2,0,1:T(8,128)S(1)} collective-permute-done((f32[64,5,1]{2,0,1:T(8,128)S(1)}, f32[64,5,1]{2,0,1:T(8,128)S(1)}, u32[]{:S(2)}, u32[]{:S(2)}) %collective-permute-start.3) | collective-permute-done | bytes 1312 | tf_op jit(solution)/shard_map/ppermute | solution.py:17
  16.6 0.0 collective-permute-done
  16.6 0.0 collective-permute-done.1
  16.6 4.5 %fusion.3.src_hbm = f32[5,8,64,128]{3,2,1,0:T(8,128)} fusion(f32[64,5,1024]{2,0,1:T(8,128)} %param.5, f32[64,5,1]{2,0,1:T(8,128)S(1)} %collective-permute-done.3, f32[64,5,1]{2,0,1:T(8,128)S(1)} %collective-permute-done.2, f32[64,5,1024]{2,0,1:T(8,128)} %param.4, f32[1,5,1024]{2,0,1:T(1,128)S(1)} %collective-permute-done.1, ...), kind=kLoop, calls=%fused_computation.4 | loop fusion | flops 2949120 | bytes 3975680 | tf_op jit(solution)/shard_map/reshape | solution.py:241
  21.0 21.6 %shard_map.46.fac_ref = f32[64,55,8,128]{3,2,1,0:T(8,128)} custom-call(f32[8,64,128]{2,1,0:T(8,128)} %bitcast.34, f32[25,8,64,128]{3,2,1,0:T(8,128)} %bitcast.31, f32[5,8,64,128]{3,2,1,0:T(8,128)} %fusion.3.src_hbm), custom_call_target="tpu_custom_call" | custom-call | tf_op jit(solution)/shard_map/pallas_call | solution.py:259
  42.6 1.1 %fusion.6 = (f32[1,55,8,128]{3,2,1,0:T(8,128)S(1)}, f32[1,55,8,128]{3,2,1,0:T(8,128)S(1)}) fusion(f32[64,55,8,128]{3,2,1,0:T(8,128)} %shard_map.46.fac_ref), kind=kLoop, calls=%fused_computation.11 | loop fusion | bytes 901120 | tf_op jit(solution)/shard_map/slice | solution.py:275
  43.7 0.2 reshape.32
  43.9 0.4 copy.8
  44.3 21.2 %all_to_all.10 = f32[16,110,64]{1,2,0:T(8,128)S(1)} all-to-all(f32[16,110,64]{1,2,0:T(8,128)S(1)} %copy.8), channel_id=1, replica_groups=mesh['line'=16,'plane'=16] {'line'}, dimensions={0} | all-to-all | bytes 901120 | tf_op jit(solution)/shard_map/all_to_all | solution.py:277
  65.5 1.3 %copy.9.ends_ref = f32[16,110,64]{2,1,0:T(8,128)} copy(f32[16,110,64]{1,2,0:T(8,128)S(1)} %all_to_all.10) | data formatting | bytes 901120 | tf_op jit(solution)/shard_map/all_to_all | solution.py:277
  66.8 5.3 %shard_map.47 = f32[16,10,64]{2,1,0:T(8,128)} custom-call(f32[16,110,64]{2,1,0:T(8,128)} %copy.9.ends_ref), custom_call_target="tpu_custom_call" | custom-call | tf_op jit(solution)/shard_map/pallas_call | solution.py:278
  72.0 1.0 %reshape.36 = f32[16,1,640]{2,1,0:T(1,128)S(1)} reshape(f32[16,10,64]{2,1,0:T(8,128)} %shard_map.47) | data formatting | bytes 81920
  73.0 11.0 %all_to_all.11 = f32[16,1,640]{2,1,0:T(1,128)S(1)} all-to-all(f32[16,1,640]{2,1,0:T(1,128)S(1)} %reshape.36), channel_id=1, replica_groups=mesh['line'=16,'plane'=16] {'line'}, dimensions={0} | all-to-all | bytes 81920 | tf_op jit(solution)/shard_map/all_to_all | solution.py:285
  84.0 0.5 broadcast
  84.5 0.7 reduce
  85.3 0.1 reshape.37
  85.4 0.7 reshape.33.bnd_ref
  86.1 8.3 %shard_map.48 = f32[5,8,64,128]{3,2,1,0:T(8,128)} custom-call(f32[64,55,8,128]{3,2,1,0:T(8,128)} %shard_map.46.fac_ref, f32[10,8,128]{2,1,0:T(8,128)} %reshape.33.bnd_ref), custom_call_target="tpu_custom_call" | custom-call | tf_op jit(solution)/shard_map/pallas_call | solution.py:288
  (2 shorter events, 0.1 us)
Async XLA Ops:
  1.0 15.5 %collective-permute-start = (f32[1,5,1024]{2,0,1:T(1,128)S(1)}, f32[1,5,1024]{2,0,1:T(1,128)S(1)}, u32[]{:S(2)}, u32[]{:S(2)}) collective-permute-start(f32[1,5,1024]{2,0,1:T(1,128)S(1)} %get-tuple-element.7), channel_id=1, source_target_pairs={{16,0},{32,16},{48,32},{64,48},{80,64},{96,80},{112,96},{128,112},... | collective-permute-start | bytes 61448 | tf_op jit(solution)/shard_map/ppermute | solution.py:20
  2.3 14.2 %collective-permute-start.1 = (f32[1,5,1024]{2,0,1:T(1,128)S(1)}, f32[1,5,1024]{2,0,1:T(1,128)S(1)}, u32[]{:S(2)}, u32[]{:S(2)}) collective-permute-start(f32[1,5,1024]{2,0,1:T(1,128)S(1)} %get-tuple-element.8), channel_id=1, source_target_pairs={{0,16},{16,32},{32,48},{48,64},{64,80},{80,96},{96,112},{112,128},... | collective-permute-start | bytes 61448 | tf_op jit(solution)/shard_map/ppermute | solution.py:17
  8.0 4.7 %collective-permute-start.2 = (f32[64,5,1]{2,0,1:T(8,128)S(1)}, f32[64,5,1]{2,0,1:T(8,128)S(1)}, u32[]{:S(2)}, u32[]{:S(2)}) collective-permute-start(f32[64,5,1]{2,0,1:T(8,128)S(1)} %get-tuple-element.9), channel_id=1, source_target_pairs={{1,0},{2,1},{3,2},{4,3},{5,4},{6,5},{7,6},{8,7},{9,8},{10,9},{11,1... | collective-permute-start | bytes 3848 | tf_op jit(solution)/shard_map/ppermute | solution.py:20
  9.9 6.6 %collective-permute-start.3 = (f32[64,5,1]{2,0,1:T(8,128)S(1)}, f32[64,5,1]{2,0,1:T(8,128)S(1)}, u32[]{:S(2)}, u32[]{:S(2)}) collective-permute-start(f32[64,5,1]{2,0,1:T(8,128)S(1)} %get-tuple-element.10), channel_id=1, source_target_pairs={{0,1},{1,2},{2,3},{3,4},{4,5},{5,6},{6,7},{7,8},{8,9},{9,10},{10,1... | collective-permute-start | bytes 3848 | tf_op jit(solution)/shard_map/ppermute | solution.py:17

commit v4 on v3

--- a/solution.py
+++ b/solution.py
@@ -179,7 +179,9 @@
     zero = jnp.zeros((1, lanes), jnp.float32)
 
     def rows_of(p, first):
-        return [ends_ref[p, first + k:first + k + 1, :] for k in range(55)]
+        if first == 0:
+            return [ends_ref[p, k:k + 1, :] for k in range(55)]
+        return [pltpu.roll(ends_ref[p, k:k + 1, :], lanes // 2, 1) for k in range(55)]
 
     def keep(q, flat):
         for k in range(60):
@@ -272,17 +274,17 @@
         compiler_params=pltpu.CompilerParams(vmem_limit_bytes=60 * 1024 * 1024),
     )(vis_s, jac_s, src_s)
 
-    ends = jnp.stack([factors[0], factors[cells - 1]]).reshape(2 * 55, parts, chunk)
-    sent = jnp.transpose(ends, (1, 0, 2))
+    ends = jnp.stack([factors[0], factors[cells - 1]]).reshape(2, 55, parts, chunk)
+    sent = jnp.transpose(ends, (2, 1, 0, 3)).reshape(parts, 55, 2 * chunk)
     gathered = lax.all_to_all(sent, "line", 0, 0, tiled=True)
     answers = pl.pallas_call(
         reduced_kernel,
-        out_shape=whole((parts, 10, chunk)),
+        out_shape=whole((parts, 10, 2 * chunk)),
         in_specs=[vmem],
         out_specs=vmem,
-        scratch_shapes=[pltpu.VMEM((parts + 1, 60, chunk), jnp.float32)],
+        scratch_shapes=[pltpu.VMEM((parts + 1, 60, 2 * chunk), jnp.float32)],
     )(gathered)
-    back = lax.all_to_all(answers, "line", 0, 0, tiled=True)
+    back = lax.all_to_all(answers[:, :, :chunk], "line", 0, 0, tiled=True)
     bounds = jnp.moveaxis(back, 1, 0).reshape(10, rows, 128)
     blocks = cells // 8
     delta_s = pl.pallas_call(

time: 94.8 us -> 94.8 us (level)
  Pallas kernels: 35.2 us -> 36.3 us
    all_to_all x2 -> x1, local copies, waits for them, and re-layouts: 1.78 us -> 0.51 us  [per_device(): back = lax.all_to_all(answers[:, :, :chunk], 'line', 0, 0, tiled=True)]
    pallas_call x1, Pallas kernels: 5.25 us -> 6.38 us  [per_device(): pl.pallas_call(reduced_kernel, out_shape=whole((parts, 10, 2 * chunk)), i...]
    reshape x1 -> x4, local copies, waits for them, and re-layouts: 0.21 us -> 1.33 us  [the longest x2 0.68 us: per_device(): jnp.stack([factors[0], factors[cells - 1]]).reshape(2, 55, parts, chunk)]
where the time goes in v4:
time: 94.8 us; the launch traced here: 94.4 us
  Pallas kernels  36.3 us (38%)
  blocking collectives  31.5 us (33%)
  starting transfers between devices  10.2 us (11%)
  local copies, waits for them, and re-layouts  6.85 us (7%)
  other arithmetic  5.22 us (6%)
  waiting for transfers between devices  4.23 us (4%)
    pallas_call x1, Pallas kernels, per_device(): pl.pallas_call(factor_kernel, out_shape=whole((cells, 55, rows, 128)), in...  21.6 us
    all_to_all x1, blocking collectives, per_device(): gathered = lax.all_to_all(sent, 'line', 0, 0, tiled=True)  20.6 us
    all_to_all x1, blocking collectives, per_device(): back = lax.all_to_all(answers[:, :, :chunk], 'line', 0, 0, tiled=True)  10.9 us
    pallas_call x1, Pallas kernels, per_device(): pl.pallas_call(combine_kernel, out_shape=whole((NV, blocks, rows * 8, 128...  8.35 us
    ppermute x2, starting transfers between devices, padded(): lax.ppermute(lax.slice_in_dim(block, block.shape[dim] - width, None, axis...  6.95 us
    pallas_call x1, Pallas kernels, per_device(): pl.pallas_call(reduced_kernel, out_shape=whole((parts, 10, 2 * chunk)), i...  6.38 us
    reshape x1, other arithmetic, stored_order(): return jnp.swapaxes(split, -3, -2).reshape(*head, cells // 8, rows * 8, 128)  4.45 us
    ppermute x2, waiting for transfers between devices, padded(): lax.ppermute(lax.slice_in_dim(block, block.shape[dim] - width, None, axis...  3.82 us
  transfers between devices with their start and end apart: 4, of which 2 were waited for; matrix products, arithmetic and copies ran while one was open for 1% of the time, Pallas kernels for 0%

profile of v4, /device:TPU:96, one launch (start us, length us, event | category | flops | bytes accessed | tf_op | source)
XLA Modules:
  0.0 94.4 jit_solution(1097039621705932820)
XLA Ops:
  0.0 1.0 %fusion.7 = (f32[1,5,1024]{2,0,1:T(1,128)S(1)}, f32[1,5,1024]{2,0,1:T(1,128)S(1)}) fusion(f32[64,5,1024]{2,0,1:T(8,128)} %param.4), kind=kLoop, calls=%fused_computation.13 | loop fusion | bytes 81920 | tf_op jit(solution)/shard_map/slice | solution.py:20
  1.0 1.3 %collective-permute-start = (f32[1,5,1024]{2,0,1:T(1,128)S(1)}, f32[1,5,1024]{2,0,1:T(1,128)S(1)}, u32[]{:S(2)}, u32[]{:S(2)}) collective-permute-start(f32[1,5,1024]{2,0,1:T(1,128)S(1)} %get-tuple-element.7), channel_id=1, source_target_pairs={{16,0},{32,16},{48,32},{64,48},{80,64},{96,80},{112,96},{128,112},... | collective-permute-start | bytes 61448 | tf_op jit(solution)/shard_map/ppermute | solution.py:20
  2.3 4.5 %collective-permute-start.1 = (f32[1,5,1024]{2,0,1:T(1,128)S(1)}, f32[1,5,1024]{2,0,1:T(1,128)S(1)}, u32[]{:S(2)}, u32[]{:S(2)}) collective-permute-start(f32[1,5,1024]{2,0,1:T(1,128)S(1)} %get-tuple-element.8), channel_id=1, source_target_pairs={{0,16},{16,32},{32,48},{48,64},{64,80},{80,96},{96,112},{112,128},... | collective-permute-start | bytes 61448 | tf_op jit(solution)/shard_map/ppermute | solution.py:17
  6.9 1.1 %fusion.8 = (f32[64,5,1]{2,0,1:T(8,128)S(1)}, f32[64,5,1]{2,0,1:T(8,128)S(1)}) fusion(f32[64,5,1024]{2,0,1:T(8,128)} %param.5), kind=kLoop, calls=%fused_computation.14 | loop fusion | bytes 5120 | tf_op jit(solution)/shard_map/slice | solution.py:20
  8.0 1.9 %collective-permute-start.2 = (f32[64,5,1]{2,0,1:T(8,128)S(1)}, f32[64,5,1]{2,0,1:T(8,128)S(1)}, u32[]{:S(2)}, u32[]{:S(2)}) collective-permute-start(f32[64,5,1]{2,0,1:T(8,128)S(1)} %get-tuple-element.9), channel_id=1, source_target_pairs={{1,0},{2,1},{3,2},{4,3},{5,4},{6,5},{7,6},{8,7},{9,8},{10,9},{11,1... | collective-permute-start | bytes 3848 | tf_op jit(solution)/shard_map/ppermute | solution.py:20
  9.9 2.4 %collective-permute-start.3 = (f32[64,5,1]{2,0,1:T(8,128)S(1)}, f32[64,5,1]{2,0,1:T(8,128)S(1)}, u32[]{:S(2)}, u32[]{:S(2)}) collective-permute-start(f32[64,5,1]{2,0,1:T(8,128)S(1)} %get-tuple-element.10), channel_id=1, source_target_pairs={{0,1},{1,2},{2,3},{3,4},{4,5},{5,6},{6,7},{7,8},{8,9},{9,10},{10,1... | collective-permute-start | bytes 3848 | tf_op jit(solution)/shard_map/ppermute | solution.py:17
  12.3 0.4 collective-permute-done.2
  12.7 3.8 %collective-permute-done.3 = f32[64,5,1]{2,0,1:T(8,128)S(1)} collective-permute-done((f32[64,5,1]{2,0,1:T(8,128)S(1)}, f32[64,5,1]{2,0,1:T(8,128)S(1)}, u32[]{:S(2)}, u32[]{:S(2)}) %collective-permute-start.3) | collective-permute-done | bytes 1312 | tf_op jit(solution)/shard_map/ppermute | solution.py:17
  16.6 0.0 collective-permute-done
  16.6 0.0 collective-permute-done.1
  16.6 4.5 %fusion.3.src_hbm = f32[5,8,64,128]{3,2,1,0:T(8,128)} fusion(f32[64,5,1024]{2,0,1:T(8,128)} %param.5, f32[64,5,1]{2,0,1:T(8,128)S(1)} %collective-permute-done.3, f32[64,5,1]{2,0,1:T(8,128)S(1)} %collective-permute-done.2, f32[64,5,1024]{2,0,1:T(8,128)} %param.4, f32[1,5,1024]{2,0,1:T(1,128)S(1)} %collective-permute-done.1, ...), kind=kLoop, calls=%fused_computation.4 | loop fusion | flops 2949120 | bytes 3975680 | tf_op jit(solution)/shard_map/reshape | solution.py:243
  21.0 21.6 %shard_map.46.fac_ref = f32[64,55,8,128]{3,2,1,0:T(8,128)} custom-call(f32[8,64,128]{2,1,0:T(8,128)} %bitcast.40, f32[25,8,64,128]{3,2,1,0:T(8,128)} %bitcast.36, f32[5,8,64,128]{3,2,1,0:T(8,128)} %fusion.3.src_hbm), custom_call_target="tpu_custom_call" | custom-call | tf_op jit(solution)/shard_map/pallas_call | solution.py:261
  42.6 1.1 %fusion.6 = (f32[1,55,8,128]{3,2,1,0:T(8,128)S(1)}, f32[1,55,8,128]{3,2,1,0:T(8,128)S(1)}) fusion(f32[64,55,8,128]{3,2,1,0:T(8,128)} %shard_map.46.fac_ref), kind=kLoop, calls=%fused_computation.12 | loop fusion | bytes 901120 | tf_op jit(solution)/shard_map/slice | solution.py:277
  43.7 0.2 reshape.35
  43.9 0.5 copy.11
  44.4 0.5 reshape.36
  44.9 0.2 copy.8
  45.1 20.6 %all_to_all.10.ends_ref = f32[16,55,128]{2,1,0:T(8,128)} all-to-all(f32[16,55,128]{2,1,0:T(8,128)S(1)} %copy.8), channel_id=1, replica_groups=mesh['line'=16,'plane'=16] {'line'}, dimensions={0} | all-to-all | bytes 901120 | tf_op jit(solution)/shard_map/all_to_all | solution.py:279
  65.6 6.4 %shard_map.47 = f32[16,10,128]{2,1,0:T(8,128)} custom-call(f32[16,55,128]{2,1,0:T(8,128)} %all_to_all.10.ends_ref), custom_call_target="tpu_custom_call" | custom-call | tf_op jit(solution)/shard_map/pallas_call | solution.py:280
  72.0 1.0 %reshape.40 = f32[16,1,640]{2,1,0:T(1,128)S(1)} reshape(f32[16,10,64]{2,1,0:T(8,128)} %bitcast.39) | data formatting | bytes 81920
  73.0 10.9 %all_to_all.11 = f32[16,1,640]{2,1,0:T(1,128)S(1)} all-to-all(f32[16,1,640]{2,1,0:T(1,128)S(1)} %reshape.40), channel_id=1, replica_groups=mesh['line'=16,'plane'=16] {'line'}, dimensions={0} | all-to-all | bytes 81920 | tf_op jit(solution)/shard_map/all_to_all | solution.py:287
  83.9 0.5 broadcast
  84.4 0.7 reduce
  85.2 0.1 reshape.41
  85.3 0.7 reshape.37.bnd_ref
  86.0 8.3 %shard_map.48 = f32[5,8,64,128]{3,2,1,0:T(8,128)} custom-call(f32[64,55,8,128]{3,2,1,0:T(8,128)} %shard_map.46.fac_ref, f32[10,8,128]{2,1,0:T(8,128)} %reshape.37.bnd_ref), custom_call_target="tpu_custom_call" | custom-call | tf_op jit(solution)/shard_map/pallas_call | solution.py:290
  (2 shorter events, 0.1 us)
Async XLA Ops:
  1.0 15.5 %collective-permute-start = (f32[1,5,1024]{2,0,1:T(1,128)S(1)}, f32[1,5,1024]{2,0,1:T(1,128)S(1)}, u32[]{:S(2)}, u32[]{:S(2)}) collective-permute-start(f32[1,5,1024]{2,0,1:T(1,128)S(1)} %get-tuple-element.7), channel_id=1, source_target_pairs={{16,0},{32,16},{48,32},{64,48},{80,64},{96,80},{112,96},{128,112},... | collective-permute-start | bytes 61448 | tf_op jit(solution)/shard_map/ppermute | solution.py:20
  2.3 14.2 %collective-permute-start.1 = (f32[1,5,1024]{2,0,1:T(1,128)S(1)}, f32[1,5,1024]{2,0,1:T(1,128)S(1)}, u32[]{:S(2)}, u32[]{:S(2)}) collective-permute-start(f32[1,5,1024]{2,0,1:T(1,128)S(1)} %get-tuple-element.8), channel_id=1, source_target_pairs={{0,16},{16,32},{32,48},{48,64},{64,80},{80,96},{96,112},{112,128},... | collective-permute-start | bytes 61448 | tf_op jit(solution)/shard_map/ppermute | solution.py:17
  8.0 4.7 %collective-permute-start.2 = (f32[64,5,1]{2,0,1:T(8,128)S(1)}, f32[64,5,1]{2,0,1:T(8,128)S(1)}, u32[]{:S(2)}, u32[]{:S(2)}) collective-permute-start(f32[64,5,1]{2,0,1:T(8,128)S(1)} %get-tuple-element.9), channel_id=1, source_target_pairs={{1,0},{2,1},{3,2},{4,3},{5,4},{6,5},{7,6},{8,7},{9,8},{10,9},{11,1... | collective-permute-start | bytes 3848 | tf_op jit(solution)/shard_map/ppermute | solution.py:20
  9.9 6.6 %collective-permute-start.3 = (f32[64,5,1]{2,0,1:T(8,128)S(1)}, f32[64,5,1]{2,0,1:T(8,128)S(1)}, u32[]{:S(2)}, u32[]{:S(2)}) collective-permute-start(f32[64,5,1]{2,0,1:T(8,128)S(1)} %get-tuple-element.10), channel_id=1, source_target_pairs={{0,1},{1,2},{2,3},{3,4},{4,5},{5,6},{6,7},{7,8},{8,9},{9,10},{10,1... | collective-permute-start | bytes 3848 | tf_op jit(solution)/shard_map/ppermute | solution.py:17

commit v5 on v3

--- a/solution.py
+++ b/solution.py
@@ -62,7 +62,10 @@
     return [x for row in grid for x in row]
 
 
-def factor_kernel(vis_hbm, jac_hbm, src_hbm, out_hbm, vis_ref, jac_ref, src_ref, out_ref, in_sem, out_sem):
+def factor_kernel(
+    edge_x, edge_lo, edge_hi, vis_hbm, jac_hbm, fx_hbm, fz_hbm, out_hbm,
+    vis_ref, jac_ref, fx_ref, fz_ref, out_ref, in_sem, out_sem,
+):
     cells = out_ref.shape[0]
     blocks = cells // 8
     tile = out_ref.shape[2:]
@@ -74,8 +77,41 @@
         return [
             pltpu.make_async_copy(vis_hbm.at[b], vis_ref.at[b], in_sem.at[0, b]),
             pltpu.make_async_copy(jac_hbm.at[:, b], jac_ref.at[:, b], in_sem.at[1, b]),
-            pltpu.make_async_copy(src_hbm.at[:, b], src_ref.at[:, b], in_sem.at[2, b]),
+            pltpu.make_async_copy(fx_hbm.at[:, b], fx_ref.at[:, b], in_sem.at[2, b]),
+            pltpu.make_async_copy(fz_hbm.at[:, b], fz_ref.at[:, b], in_sem.at[3, b]),
         ]
+
+    lane = lax.broadcasted_iota(jnp.int32, tile, 1)
+    row = lax.broadcasted_iota(jnp.int32, tile, 0)
+    lane_up = pltpu.roll(lane, 127, 1) == (lane + 1) % 128
+    row_up = pltpu.roll(row, rows - 1, 0) == (row + 1) % rows
+
+    def following(x):
+        ahead = jnp.where(lane_up, pltpu.roll(x, 127, 1), pltpu.roll(x, 1, 1))
+        wrapped = jnp.where(row_up, pltpu.roll(ahead, rows - 1, 0), pltpu.roll(ahead, 1, 0))
+        return jnp.where(lane == 127, wrapped, ahead)
+
+    def preceding(x):
+        behind = jnp.where(lane_up, pltpu.roll(x, 1, 1), pltpu.roll(x, 127, 1))
+        wrapped = jnp.where(row_up, pltpu.roll(behind, 1, 0), pltpu.roll(behind, rows - 1, 0))
+        return jnp.where(lane == 0, wrapped, behind)
+
+    last_line = (lane == 127) & (row == rows - 1)
+    first_line = (lane == 0) & (row == 0)
+
+    def source_of(i, block, picked, a):
+        low = jnp.maximum(i - 1, 0)
+        high = jnp.minimum(i + 1, cells - 1)
+        below = fx_ref[a, low // 8, pl.ds(low % 8, rows, stride=8), :]
+        above = fx_ref[a, high // 8, pl.ds(high % 8, rows, stride=8), :]
+        is_first = (i == 0).astype(jnp.float32)
+        is_last = (i == cells - 1).astype(jnp.float32)
+        below = (1.0 - is_first) * below + is_first * edge_x[0, a]
+        above = (1.0 - is_last) * above + is_last * edge_x[1, a]
+        across = fz_ref[a, block, picked, :]
+        nxt = jnp.where(last_line, edge_hi[a, i], following(across))
+        prv = jnp.where(first_line, edge_lo[a, i], preceding(across))
+        return -0.5 * courant * (above - below) - 0.5 * courant * (nxt - prv)
 
     def departure(b):
         return pltpu.make_async_copy(out_ref.at[pl.ds(b * 8, 8)], out_hbm.at[pl.ds(b * 8, 8)], out_sem.at[b])
@@ -83,11 +119,13 @@
     for b in range(blocks):
         for copy in arrivals(b):
             copy.start()
+    for copy in arrivals(0):
+        copy.wait()
 
     def forward(i, carry):
-        @pl.when(i % 8 == 0)
+        @pl.when((i % 8 == 0) & (i + 8 < cells))
         def _():
-            for copy in arrivals(i // 8):
+            for copy in arrivals(i // 8 + 1):
                 copy.wait()
 
         c_prev = grid_of(carry[0:25], NV, NV)
@@ -106,7 +144,7 @@
         lw = matmul(lower, w_prev, NV, NV, NV)
         cols = []
         for a in range(NV):
-            cols.append(upper[a] + [src_ref[a, block, picked, :] - lg[a][0]] + [-x for x in lw[a]])
+            cols.append(upper[a] + [source_of(i, block, picked, a) - lg[a][0]] + [-x for x in lw[a]])
         sol = gauss_jordan(schur, cols)
         c_new = [row[0:NV] for row in sol]
         g_new = [row[NV] for row in sol]
@@ -248,29 +286,32 @@
     chunk = line_count // parts
     stream = padded(flux_x, (("line", 0),), 1)
     across = padded(flux_z, (("plane", 2),), 1)
-    source = -0.5 * courant * (stream[2:] - stream[:-2]) - 0.5 * courant * (
-        across[:, :, 2:] - across[:, :, :-2]
-    )
-    src_s = stored_order(jnp.transpose(source, (1, 0, 2)), 1)
+    edge_x = jnp.stack([stream[0], stream[cells + 1]]).reshape(2, NV, rows, 128)
+    edge_lo = jnp.transpose(across[:, :, 0])
+    edge_hi = jnp.transpose(across[:, :, line_count + 1])
+    fx_s = stored_order(jnp.transpose(flux_x, (1, 0, 2)), 1)
+    fz_s = stored_order(jnp.transpose(flux_z, (1, 0, 2)), 1)
     jac_s = stored_order(jnp.transpose(jacobian, (1, 2, 0, 3)).reshape(NV * NV, cells, line_count), 1)
     vis_s = stored_order(viscous, 0)
     vmem = pl.BlockSpec(memory_space=pltpu.VMEM)
     hbm = pl.BlockSpec(memory_space=pl.ANY)
+    smem = pl.BlockSpec(memory_space=pltpu.SMEM)
     factors = pl.pallas_call(
         factor_kernel,
         out_shape=whole((cells, 55, rows, 128)),
-        in_specs=[hbm, hbm, hbm],
+        in_specs=[vmem, smem, smem, hbm, hbm, hbm, hbm],
         out_specs=hbm,
         scratch_shapes=[
             pltpu.VMEM(vis_s.shape, jnp.float32),
             pltpu.VMEM(jac_s.shape, jnp.float32),
-            pltpu.VMEM(src_s.shape, jnp.float32),
+            pltpu.VMEM(fx_s.shape, jnp.float32),
+            pltpu.VMEM(fz_s.shape, jnp.float32),
             pltpu.VMEM((cells, 55, rows, 128), jnp.float32),
-            pltpu.SemaphoreType.DMA((3, cells // 8)),
+            pltpu.SemaphoreType.DMA((4, cells // 8)),
             pltpu.SemaphoreType.DMA((cells // 8,)),
         ],
         compiler_params=pltpu.CompilerParams(vmem_limit_bytes=60 * 1024 * 1024),
-    )(vis_s, jac_s, src_s)
+    )(edge_x, edge_lo, edge_hi, vis_s, jac_s, fx_s, fz_s)
 
     ends = jnp.stack([factors[0], factors[cells - 1]]).reshape(2 * 55, parts, chunk)
     sent = jnp.transpose(ends, (1, 0, 2))

time: 94.8 us -> 91 us (0.960)
  the two profiles are of different devices: /device:TPU:96 before, /device:TPU:160 now
where the time goes in v5:
time: 91 us; the launch traced here: 90.5 us
  Pallas kernels  38.1 us (42%)
  blocking collectives  31.6 us (35%)
  starting transfers between devices  10.3 us (11%)
  local copies, waits for them, and re-layouts  8.88 us (10%)
    pallas_call x1, Pallas kernels, per_device(): pl.pallas_call(factor_kernel, out_shape=whole((cells, 55, rows, 128)), in...  24.5 us
    all_to_all x1, blocking collectives, per_device(): gathered = lax.all_to_all(sent, 'line', 0, 0, tiled=True)  20.6 us
    all_to_all x1, blocking collectives, per_device(): back = lax.all_to_all(answers, 'line', 0, 0, tiled=True)  11 us
    pallas_call x1, Pallas kernels, per_device(): pl.pallas_call(combine_kernel, out_shape=whole((NV, blocks, rows * 8, 128...  8.35 us
    ppermute x2, starting transfers between devices, padded(): lax.ppermute(lax.slice_in_dim(block, block.shape[dim] - width, None, axis...  5.4 us
    pallas_call x1, Pallas kernels, per_device(): pl.pallas_call(reduced_kernel, out_shape=whole((parts, 10, chunk)), in_sp...  5.24 us
    ppermute x2, starting transfers between devices, padded(): lax.ppermute(lax.slice_in_dim(block, 0, width, axis=dim), axis, backward)  4.94 us
    unnamed x10, local copies, waits for them, and re-layouts  1.94 us
  transfers between devices with their start and end apart: 4, of which 1 were waited for; matrix products, arithmetic and copies ran while one was open for 2% of the time, Pallas kernels for 0%

profile of v5, /device:TPU:160, one launch (start us, length us, event | category | flops | bytes accessed | tf_op | source)
XLA Modules:
  0.0 90.5 jit_solution(5919142731425157868)
XLA Ops:
  0.0 1.0 %fusion.2 = (f32[1,5,1024]{2,0,1:T(1,128)S(1)}, f32[1,5,1024]{2,0,1:T(1,128)S(1)}) fusion(f32[64,5,1024]{2,0,1:T(8,128)} %param.4), kind=kLoop, calls=%fused_computation.4 | loop fusion | bytes 81920 | tf_op jit(solution)/shard_map/slice | solution.py:18
  1.0 3.5 %collective-permute-start = (f32[1,5,1024]{2,1,0:T(8,128)S(1)}, f32[1,5,1024]{2,1,0:T(8,128)S(1)}, u32[]{:S(2)}, u32[]{:S(2)}) collective-permute-start(f32[1,5,1024]{2,1,0:T(8,128)S(1)} %copy.24), channel_id=1, source_target_pairs={{0,16},{16,32},{32,48},{48,64},{64,80},{80,96},{96,112},{112,128},... | collective-permute-start | bytes 61448 | tf_op jit(solution)/shard_map/ppermute | solution.py:17
  4.5 1.3 %collective-permute-start.1 = (f32[1,5,1024]{2,1,0:T(8,128)S(1)}, f32[1,5,1024]{2,1,0:T(8,128)S(1)}, u32[]{:S(2)}, u32[]{:S(2)}) collective-permute-start(f32[1,5,1024]{2,1,0:T(8,128)S(1)} %copy.25), channel_id=1, source_target_pairs={{16,0},{32,16},{48,32},{64,48},{80,64},{96,80},{112,96},{128,112},... | collective-permute-start | bytes 61448 | tf_op jit(solution)/shard_map/ppermute | solution.py:20
  5.8 1.1 %fusion.1 = (f32[64,5,1]{2,0,1:T(8,128)S(1)}, f32[64,5,1]{2,0,1:T(8,128)S(1)}) fusion(f32[64,5,1024]{2,0,1:T(8,128)} %param.5), kind=kLoop, calls=%fused_computation.3 | loop fusion | bytes 5120 | tf_op jit(solution)/shard_map/slice | solution.py:20
  7.0 0.1 copy.26
  7.1 1.9 %collective-permute-start.2 = (f32[64,5,1]{0,1,2:T(8,128)S(1)}, f32[64,5,1]{0,1,2:T(8,128)S(1)}, u32[]{:S(2)}, u32[]{:S(2)}) collective-permute-start(f32[64,5,1]{0,1,2:T(8,128)S(1)} %copy.26), channel_id=1, source_target_pairs={{0,1},{1,2},{2,3},{3,4},{4,5},{5,6},{6,7},{7,8},{8,9},{9,10},{10,1... | collective-permute-start | bytes 3848 | tf_op jit(solution)/shard_map/ppermute | solution.py:17
  9.0 0.1 copy.27
  9.1 3.6 %collective-permute-start.3 = (f32[64,5,1]{0,1,2:T(8,128)S(1)}, f32[64,5,1]{0,1,2:T(8,128)S(1)}, u32[]{:S(2)}, u32[]{:S(2)}) collective-permute-start(f32[64,5,1]{0,1,2:T(8,128)S(1)} %copy.27), channel_id=1, source_target_pairs={{1,0},{2,1},{3,2},{4,3},{5,4},{6,5},{7,6},{8,7},{9,8},{10,9},{11,1... | collective-permute-start | bytes 3848 | tf_op jit(solution)/shard_map/ppermute | solution.py:20
  12.8 0.0 collective-permute-done
  12.8 0.0 collective-permute-done.1
  12.8 0.6 reshape.48.edge_x
  13.5 0.0 collective-permute-done.2
  13.5 0.0 copy-start
  13.5 0.6 collective-permute-done.3
  14.1 0.0 copy-start.1
  14.1 0.0 copy-done
  14.1 0.6 copy-done.1
  14.7 24.5 %shard_map.46.fac_ref = f32[64,55,8,128]{3,2,1,0:T(8,128)} custom-call(f32[2,5,8,128]{3,2,1,0:T(8,128)} %reshape.48.edge_x, f32[5,64]{1,0:T(8,128)} %bitcast.49, f32[5,64]{1,0:T(8,128)} %bitcast.50, f32[8,64,128]{2,1,0:T(8,128)} %bitcast.48, f32[25,8,64,128]{3,2,1,0:T(8,128)} %bitcast.43, f32[5,8,64,128]{3,2,1,0:T(8,128)} %bitcast.46, f32[5,8,64,128]{3,2,1,0:T(8,128)} %bitcast.45), custom_call_target="tpu_custom_call" | custom-call | tf_op jit(solution)/shard_map/pallas_call | solution.py:299
  39.2 1.1 %fusion = (f32[1,55,8,128]{3,2,1,0:T(8,128)S(1)}, f32[1,55,8,128]{3,2,1,0:T(8,128)S(1)}) fusion(f32[64,55,8,128]{3,2,1,0:T(8,128)} %shard_map.46.fac_ref), kind=kLoop, calls=%fused_computation.2 | loop fusion | bytes 901120 | tf_op jit(solution)/shard_map/slice | solution.py:316
  40.3 0.2 reshape.44
  40.6 0.4 copy.20
  41.0 20.6 %all_to_all.10 = f32[16,110,64]{1,2,0:T(8,128)S(1)} all-to-all(f32[16,110,64]{1,2,0:T(8,128)S(1)} %copy.20), channel_id=1, replica_groups=mesh['line'=16,'plane'=16] {'line'}, dimensions={0} | all-to-all | bytes 901120 | tf_op jit(solution)/shard_map/all_to_all | solution.py:318
  61.6 1.3 %copy.21.ends_ref = f32[16,110,64]{2,1,0:T(8,128)} copy(f32[16,110,64]{1,2,0:T(8,128)S(1)} %all_to_all.10) | data formatting | bytes 901120 | tf_op jit(solution)/shard_map/all_to_all | solution.py:318
  62.9 5.2 %shard_map.47 = f32[16,10,64]{2,1,0:T(8,128)} custom-call(f32[16,110,64]{2,1,0:T(8,128)} %copy.21.ends_ref), custom_call_target="tpu_custom_call" | custom-call | tf_op jit(solution)/shard_map/pallas_call | solution.py:319
  68.1 1.0 %reshape.49 = f32[16,1,640]{2,1,0:T(1,128)S(1)} reshape(f32[16,10,64]{2,1,0:T(8,128)} %shard_map.47) | data formatting | bytes 81920
  69.1 11.0 %all_to_all.11 = f32[16,1,640]{2,1,0:T(1,128)S(1)} all-to-all(f32[16,1,640]{2,1,0:T(1,128)S(1)} %reshape.49), channel_id=1, replica_groups=mesh['line'=16,'plane'=16] {'line'}, dimensions={0} | all-to-all | bytes 81920 | tf_op jit(solution)/shard_map/all_to_all | solution.py:326
  80.1 0.5 broadcast
  80.6 0.7 reduce
  81.4 0.1 reshape.50
  81.5 0.7 reshape.45.bnd_ref
  82.2 8.3 %shard_map.48 = f32[5,8,64,128]{3,2,1,0:T(8,128)} custom-call(f32[64,55,8,128]{3,2,1,0:T(8,128)} %shard_map.46.fac_ref, f32[10,8,128]{2,1,0:T(8,128)} %reshape.45.bnd_ref), custom_call_target="tpu_custom_call" | custom-call | tf_op jit(solution)/shard_map/pallas_call | solution.py:329
  (5 shorter events, 0.1 us)
Async XLA Ops:
  1.0 11.8 %collective-permute-start = (f32[1,5,1024]{2,1,0:T(8,128)S(1)}, f32[1,5,1024]{2,1,0:T(8,128)S(1)}, u32[]{:S(2)}, u32[]{:S(2)}) collective-permute-start(f32[1,5,1024]{2,1,0:T(8,128)S(1)} %copy.24), channel_id=1, source_target_pairs={{0,16},{16,32},{32,48},{48,64},{64,80},{80,96},{96,112},{112,128},... | collective-permute-start | bytes 61448 | tf_op jit(solution)/shard_map/ppermute | solution.py:17
  4.5 8.3 %collective-permute-start.1 = (f32[1,5,1024]{2,1,0:T(8,128)S(1)}, f32[1,5,1024]{2,1,0:T(8,128)S(1)}, u32[]{:S(2)}, u32[]{:S(2)}) collective-permute-start(f32[1,5,1024]{2,1,0:T(8,128)S(1)} %copy.25), channel_id=1, source_target_pairs={{16,0},{32,16},{48,32},{64,48},{80,64},{96,80},{112,96},{128,112},... | collective-permute-start | bytes 61448 | tf_op jit(solution)/shard_map/ppermute | solution.py:20
  7.1 6.4 %collective-permute-start.2 = (f32[64,5,1]{0,1,2:T(8,128)S(1)}, f32[64,5,1]{0,1,2:T(8,128)S(1)}, u32[]{:S(2)}, u32[]{:S(2)}) collective-permute-start(f32[64,5,1]{0,1,2:T(8,128)S(1)} %copy.26), channel_id=1, source_target_pairs={{0,1},{1,2},{2,3},{3,4},{4,5},{5,6},{6,7},{7,8},{8,9},{9,10},{10,1... | collective-permute-start | bytes 3848 | tf_op jit(solution)/shard_map/ppermute | solution.py:17
  9.1 5.0 %collective-permute-start.3 = (f32[64,5,1]{0,1,2:T(8,128)S(1)}, f32[64,5,1]{0,1,2:T(8,128)S(1)}, u32[]{:S(2)}, u32[]{:S(2)}) collective-permute-start(f32[64,5,1]{0,1,2:T(8,128)S(1)} %copy.27), channel_id=1, source_target_pairs={{1,0},{2,1},{3,2},{4,3},{5,4},{6,5},{7,6},{8,7},{9,8},{10,9},{11,1... | collective-permute-start | bytes 3848 | tf_op jit(solution)/shard_map/ppermute | solution.py:20
  13.5 0.6 copy-start
  14.1 0.6 copy-start.1

commit v6 on v5

--- a/solution.py
+++ b/solution.py
@@ -86,15 +86,14 @@
     lane_up = pltpu.roll(lane, 127, 1) == (lane + 1) % 128
     row_up = pltpu.roll(row, rows - 1, 0) == (row + 1) % rows
 
-    def following(x):
-        ahead = jnp.where(lane_up, pltpu.roll(x, 127, 1), pltpu.roll(x, 1, 1))
-        wrapped = jnp.where(row_up, pltpu.roll(ahead, rows - 1, 0), pltpu.roll(ahead, 1, 0))
-        return jnp.where(lane == 127, wrapped, ahead)
-
-    def preceding(x):
-        behind = jnp.where(lane_up, pltpu.roll(x, 1, 1), pltpu.roll(x, 127, 1))
-        wrapped = jnp.where(row_up, pltpu.roll(behind, 1, 0), pltpu.roll(behind, rows - 1, 0))
-        return jnp.where(lane == 0, wrapped, behind)
+    def neighbours(x):
+        left = pltpu.roll(x, 127, 1)
+        right = pltpu.roll(x, 1, 1)
+        ahead = jnp.where(lane_up, left, right)
+        behind = jnp.where(lane_up, right, left)
+        ahead_wrap = jnp.where(row_up, pltpu.roll(ahead, rows - 1, 0), pltpu.roll(ahead, 1, 0))
+        behind_wrap = jnp.where(row_up, pltpu.roll(behind, 1, 0), pltpu.roll(behind, rows - 1, 0))
+        return jnp.where(lane == 127, ahead_wrap, ahead), jnp.where(lane == 0, behind_wrap, behind)
 
     last_line = (lane == 127) & (row == rows - 1)
     first_line = (lane == 0) & (row == 0)
@@ -109,8 +108,9 @@
         below = (1.0 - is_first) * below + is_first * edge_x[0, a]
         above = (1.0 - is_last) * above + is_last * edge_x[1, a]
         across = fz_ref[a, block, picked, :]
-        nxt = jnp.where(last_line, edge_hi[a, i], following(across))
-        prv = jnp.where(first_line, edge_lo[a, i], preceding(across))
+        following, preceding = neighbours(across)
+        nxt = jnp.where(last_line, edge_hi[a, i], following)
+        prv = jnp.where(first_line, edge_lo[a, i], preceding)
         return -0.5 * courant * (above - below) - 0.5 * courant * (nxt - prv)
 
     def departure(b):

time: 91 us -> 91 us (level)
  no operation moved by 1% of the time
where the time goes in v6:
time: 91 us; the launch traced here: 90.6 us
  Pallas kernels  38.2 us (42%)
  blocking collectives  31.6 us (35%)
  starting transfers between devices  10.3 us (11%)
  local copies, waits for them, and re-layouts  8.88 us (10%)
    pallas_call x1, Pallas kernels, per_device(): pl.pallas_call(factor_kernel, out_shape=whole((cells, 55, rows, 128)), in...  24.6 us
    all_to_all x1, blocking collectives, per_device(): gathered = lax.all_to_all(sent, 'line', 0, 0, tiled=True)  20.6 us
    all_to_all x1, blocking collectives, per_device(): back = lax.all_to_all(answers, 'line', 0, 0, tiled=True)  11 us
    pallas_call x1, Pallas kernels, per_device(): pl.pallas_call(combine_kernel, out_shape=whole((NV, blocks, rows * 8, 128...  8.35 us
    ppermute x2, starting transfers between devices, padded(): lax.ppermute(lax.slice_in_dim(block, block.shape[dim] - width, None, axis...  5.4 us
    pallas_call x1, Pallas kernels, per_device(): pl.pallas_call(reduced_kernel, out_shape=whole((parts, 10, chunk)), in_sp...  5.24 us
    ppermute x2, starting transfers between devices, padded(): lax.ppermute(lax.slice_in_dim(block, 0, width, axis=dim), axis, backward)  4.94 us
    unnamed x10, local copies, waits for them, and re-layouts  1.94 us
  transfers between devices with their start and end apart: 4, of which 1 were waited for; matrix products, arithmetic and copies ran while one was open for 2% of the time, Pallas kernels for 0%

profile of v6, /device:TPU:160, one launch (start us, length us, event | category | flops | bytes accessed | tf_op | source)
XLA Modules:
  0.0 90.6 jit_solution(504857383863632296)
XLA Ops:
  0.0 1.0 %fusion.2 = (f32[1,5,1024]{2,0,1:T(1,128)S(1)}, f32[1,5,1024]{2,0,1:T(1,128)S(1)}) fusion(f32[64,5,1024]{2,0,1:T(8,128)} %param.4), kind=kLoop, calls=%fused_computation.4 | loop fusion | bytes 81920 | tf_op jit(solution)/shard_map/slice | solution.py:18
  1.0 3.5 %collective-permute-start = (f32[1,5,1024]{2,1,0:T(8,128)S(1)}, f32[1,5,1024]{2,1,0:T(8,128)S(1)}, u32[]{:S(2)}, u32[]{:S(2)}) collective-permute-start(f32[1,5,1024]{2,1,0:T(8,128)S(1)} %copy.24), channel_id=1, source_target_pairs={{0,16},{16,32},{32,48},{48,64},{64,80},{80,96},{96,112},{112,128},... | collective-permute-start | bytes 61448 | tf_op jit(solution)/shard_map/ppermute | solution.py:17
  4.5 1.3 %collective-permute-start.1 = (f32[1,5,1024]{2,1,0:T(8,128)S(1)}, f32[1,5,1024]{2,1,0:T(8,128)S(1)}, u32[]{:S(2)}, u32[]{:S(2)}) collective-permute-start(f32[1,5,1024]{2,1,0:T(8,128)S(1)} %copy.25), channel_id=1, source_target_pairs={{16,0},{32,16},{48,32},{64,48},{80,64},{96,80},{112,96},{128,112},... | collective-permute-start | bytes 61448 | tf_op jit(solution)/shard_map/ppermute | solution.py:20
  5.8 1.1 %fusion.1 = (f32[64,5,1]{2,0,1:T(8,128)S(1)}, f32[64,5,1]{2,0,1:T(8,128)S(1)}) fusion(f32[64,5,1024]{2,0,1:T(8,128)} %param.5), kind=kLoop, calls=%fused_computation.3 | loop fusion | bytes 5120 | tf_op jit(solution)/shard_map/slice | solution.py:20
  7.0 0.1 copy.26
  7.1 1.9 %collective-permute-start.2 = (f32[64,5,1]{0,1,2:T(8,128)S(1)}, f32[64,5,1]{0,1,2:T(8,128)S(1)}, u32[]{:S(2)}, u32[]{:S(2)}) collective-permute-start(f32[64,5,1]{0,1,2:T(8,128)S(1)} %copy.26), channel_id=1, source_target_pairs={{0,1},{1,2},{2,3},{3,4},{4,5},{5,6},{6,7},{7,8},{8,9},{9,10},{10,1... | collective-permute-start | bytes 3848 | tf_op jit(solution)/shard_map/ppermute | solution.py:17
  9.0 0.1 copy.27
  9.1 3.6 %collective-permute-start.3 = (f32[64,5,1]{0,1,2:T(8,128)S(1)}, f32[64,5,1]{0,1,2:T(8,128)S(1)}, u32[]{:S(2)}, u32[]{:S(2)}) collective-permute-start(f32[64,5,1]{0,1,2:T(8,128)S(1)} %copy.27), channel_id=1, source_target_pairs={{1,0},{2,1},{3,2},{4,3},{5,4},{6,5},{7,6},{8,7},{9,8},{10,9},{11,1... | collective-permute-start | bytes 3848 | tf_op jit(solution)/shard_map/ppermute | solution.py:20
  12.8 0.0 collective-permute-done
  12.8 0.0 collective-permute-done.1
  12.8 0.6 reshape.48.edge_x
  13.5 0.0 collective-permute-done.2
  13.5 0.0 copy-start
  13.5 0.6 collective-permute-done.3
  14.1 0.0 copy-start.1
  14.1 0.0 copy-done
  14.1 0.6 copy-done.1
  14.7 24.6 %shard_map.46.fac_ref = f32[64,55,8,128]{3,2,1,0:T(8,128)} custom-call(f32[2,5,8,128]{3,2,1,0:T(8,128)} %reshape.48.edge_x, f32[5,64]{1,0:T(8,128)} %bitcast.49, f32[5,64]{1,0:T(8,128)} %bitcast.50, f32[8,64,128]{2,1,0:T(8,128)} %bitcast.48, f32[25,8,64,128]{3,2,1,0:T(8,128)} %bitcast.43, f32[5,8,64,128]{3,2,1,0:T(8,128)} %bitcast.46, f32[5,8,64,128]{3,2,1,0:T(8,128)} %bitcast.45), custom_call_target="tpu_custom_call" | custom-call | tf_op jit(solution)/shard_map/pallas_call | solution.py:299
  39.3 1.1 %fusion = (f32[1,55,8,128]{3,2,1,0:T(8,128)S(1)}, f32[1,55,8,128]{3,2,1,0:T(8,128)S(1)}) fusion(f32[64,55,8,128]{3,2,1,0:T(8,128)} %shard_map.46.fac_ref), kind=kLoop, calls=%fused_computation.2 | loop fusion | bytes 901120 | tf_op jit(solution)/shard_map/slice | solution.py:316
  40.4 0.2 reshape.44
  40.6 0.4 copy.20
  41.0 20.6 %all_to_all.10 = f32[16,110,64]{1,2,0:T(8,128)S(1)} all-to-all(f32[16,110,64]{1,2,0:T(8,128)S(1)} %copy.20), channel_id=1, replica_groups=mesh['line'=16,'plane'=16] {'line'}, dimensions={0} | all-to-all | bytes 901120 | tf_op jit(solution)/shard_map/all_to_all | solution.py:318
  61.6 1.3 %copy.21.ends_ref = f32[16,110,64]{2,1,0:T(8,128)} copy(f32[16,110,64]{1,2,0:T(8,128)S(1)} %all_to_all.10) | data formatting | bytes 901120 | tf_op jit(solution)/shard_map/all_to_all | solution.py:318
  62.9 5.2 %shard_map.47 = f32[16,10,64]{2,1,0:T(8,128)} custom-call(f32[16,110,64]{2,1,0:T(8,128)} %copy.21.ends_ref), custom_call_target="tpu_custom_call" | custom-call | tf_op jit(solution)/shard_map/pallas_call | solution.py:319
  68.2 1.0 %reshape.49 = f32[16,1,640]{2,1,0:T(1,128)S(1)} reshape(f32[16,10,64]{2,1,0:T(8,128)} %shard_map.47) | data formatting | bytes 81920
  69.2 11.0 %all_to_all.11 = f32[16,1,640]{2,1,0:T(1,128)S(1)} all-to-all(f32[16,1,640]{2,1,0:T(1,128)S(1)} %reshape.49), channel_id=1, replica_groups=mesh['line'=16,'plane'=16] {'line'}, dimensions={0} | all-to-all | bytes 81920 | tf_op jit(solution)/shard_map/all_to_all | solution.py:326
  80.1 0.5 broadcast
  80.7 0.7 reduce
  81.4 0.1 reshape.50
  81.5 0.7 reshape.45.bnd_ref
  82.2 8.3 %shard_map.48 = f32[5,8,64,128]{3,2,1,0:T(8,128)} custom-call(f32[64,55,8,128]{3,2,1,0:T(8,128)} %shard_map.46.fac_ref, f32[10,8,128]{2,1,0:T(8,128)} %reshape.45.bnd_ref), custom_call_target="tpu_custom_call" | custom-call | tf_op jit(solution)/shard_map/pallas_call | solution.py:329
  (5 shorter events, 0.1 us)
Async XLA Ops:
  1.0 11.8 %collective-permute-start = (f32[1,5,1024]{2,1,0:T(8,128)S(1)}, f32[1,5,1024]{2,1,0:T(8,128)S(1)}, u32[]{:S(2)}, u32[]{:S(2)}) collective-permute-start(f32[1,5,1024]{2,1,0:T(8,128)S(1)} %copy.24), channel_id=1, source_target_pairs={{0,16},{16,32},{32,48},{48,64},{64,80},{80,96},{96,112},{112,128},... | collective-permute-start | bytes 61448 | tf_op jit(solution)/shard_map/ppermute | solution.py:17
  4.5 8.3 %collective-permute-start.1 = (f32[1,5,1024]{2,1,0:T(8,128)S(1)}, f32[1,5,1024]{2,1,0:T(8,128)S(1)}, u32[]{:S(2)}, u32[]{:S(2)}) collective-permute-start(f32[1,5,1024]{2,1,0:T(8,128)S(1)} %copy.25), channel_id=1, source_target_pairs={{16,0},{32,16},{48,32},{64,48},{80,64},{96,80},{112,96},{128,112},... | collective-permute-start | bytes 61448 | tf_op jit(solution)/shard_map/ppermute | solution.py:20
  7.1 6.4 %collective-permute-start.2 = (f32[64,5,1]{0,1,2:T(8,128)S(1)}, f32[64,5,1]{0,1,2:T(8,128)S(1)}, u32[]{:S(2)}, u32[]{:S(2)}) collective-permute-start(f32[64,5,1]{0,1,2:T(8,128)S(1)} %copy.26), channel_id=1, source_target_pairs={{0,1},{1,2},{2,3},{3,4},{4,5},{5,6},{6,7},{7,8},{8,9},{9,10},{10,1... | collective-permute-start | bytes 3848 | tf_op jit(solution)/shard_map/ppermute | solution.py:17
  9.1 5.0 %collective-permute-start.3 = (f32[64,5,1]{0,1,2:T(8,128)S(1)}, f32[64,5,1]{0,1,2:T(8,128)S(1)}, u32[]{:S(2)}, u32[]{:S(2)}) collective-permute-start(f32[64,5,1]{0,1,2:T(8,128)S(1)} %copy.27), channel_id=1, source_target_pairs={{1,0},{2,1},{3,2},{4,3},{5,4},{6,5},{7,6},{8,7},{9,8},{10,9},{11,1... | collective-permute-start | bytes 3848 | tf_op jit(solution)/shard_map/ppermute | solution.py:20
  13.5 0.6 copy-start
  14.1 0.6 copy-start.1
